TPU v7x, 128 devices: a whole 4x4x4 slice. The times are simulated.
128 devices in a mesh: dp: 16 (over x_lo, z, core), tensor: 8 (over y, x_hi).
Axes of the slice: x: 4 (x_hi: 2, x_lo: 2; x = x_hi * 2 + x_lo), y: 4, z: 4, core: 2. Of those that a mesh axis runs over, the one named last changes fastest.
Arguments:
- tokens: bfloat16 [12288, 1024], P('dp'), may hold values from -72 to 72
- w_qkv: float32 [1024, 3072], P(('dp', 'tensor')), may hold values from -0.1875 to 0.1875
- w_out: float32 [1024, 1024], P(None, ('dp', 'tensor')), may hold values from -0.1875 to 0.1875
- w_up: float32 [1024, 4096], P(('dp', 'tensor')), may hold values from -0.1875 to 0.1875
- w_down: float32 [4096, 1024], P(None, ('dp', 'tensor')), may hold values from -0.09375 to 0.09375
- slot_request: int32 [96, 128], replicated, may hold values from -1 to 3, as said below
Outputs:
- encoded: bfloat16 [12288, 1024], P('dp')
Inputs may be any that keep to these rules, and one draw needn't show every extreme that they name: `slot_request`: requests are numbered 0 to 3, all present; each request holds 1 to 48 pages and one holds exactly 48; each request's pages are full except its last page, whose empty slots are its final ones; pages may sit in any slot of the table.
All inputs are finite; a program needn't handle non-finite values.
Results may differ from a plain program's by a relative error of at most 0.025.
The roundings to bfloat16 on the way count: a program that leaves them out, or rounds other values in their place, can miss the bound.
Values may be sent and summed in bfloat16 or wider, within the bound.
No kernel may reach another device: no remote copies, remote signals or barrier semaphores. Data moves between devices by JAX's collectives and lax.ppermute only.
A program may use at most 128 MiB of HBM per device.

v0:
```python
import math

import jax
import jax.numpy as jnp
from jax import lax
from jax.experimental import pallas as pl
from jax.experimental.pallas import tpu as pltpu
from jax.sharding import PartitionSpec as P

D = 1024
H = 16


def layer_norm(value):
    mean = jnp.mean(value, axis=-1, keepdims=True)
    centred = value - mean
    spread = jnp.mean(centred * centred, axis=-1, keepdims=True)
    return centred * lax.rsqrt(spread + 1e-05)


def spread_weights(w_qkv, w_out, w_up, w_down):
    groups = lax.axis_size("tensor")
    qkv = w_qkv.astype(jnp.bfloat16)
    up = w_up.astype(jnp.bfloat16)
    out = w_out.astype(jnp.bfloat16)
    down = w_down.astype(jnp.bfloat16)
    rows = qkv.shape[0]
    parts = [
        qkv.reshape(rows, groups, -1).transpose(1, 0, 2).reshape(groups, -1),
        up.reshape(rows, groups, -1).transpose(1, 0, 2).reshape(groups, -1),
        down.reshape(groups, -1),
        jnp.broadcast_to(out.reshape(1, -1), (groups, out.size)),
    ]
    sizes = [p.shape[1] for p in parts]
    got = lax.all_to_all(jnp.concatenate(parts, axis=1), "tensor", 0, 0, tiled=True)
    cut = [sum(sizes[:k]) for k in range(5)]
    piece = [got[:, cut[k]:cut[k + 1]] for k in range(4)]
    qkv_local = piece[0].reshape(groups * rows, -1)
    up_local = piece[1].reshape(groups * rows, -1)
    down_rows = down.shape[0] // groups
    down_local = piece[2].reshape(groups, down_rows, -1).transpose(1, 0, 2).reshape(down_rows, -1)
    out_local = piece[3].reshape(groups, out.shape[0], -1).transpose(1, 0, 2).reshape(out.shape[0], -1)
    qkv_block = lax.all_gather(qkv_local, "dp", axis=0, tiled=True)
    rest = [up_local, down_local, out_local]
    flat = jnp.concatenate([r.reshape(-1) for r in rest])
    all_flat = lax.all_gather(flat, "dp", axis=0, tiled=False)
    dp_size = all_flat.shape[0]
    offs = [0, up_local.size, up_local.size + down_local.size, flat.shape[0]]
    up_block = all_flat[:, offs[0]:offs[1]].reshape(dp_size * up_local.shape[0], -1)
    down_block = (
        all_flat[:, offs[1]:offs[2]].reshape(dp_size, *down_local.shape).transpose(1, 0, 2).reshape(down_rows, -1)
    )
    out_full = (
        all_flat[:, offs[2]:offs[3]].reshape(dp_size, *out_local.shape).transpose(1, 0, 2).reshape(out.shape[0], -1)
    )
    return qkv_block, up_block, down_block, out_full


def sum_scatter(part):
    groups = lax.axis_size("tensor")
    pieces = lax.all_to_all(part.reshape(groups, -1, part.shape[1]), "tensor", 0, 0, tiled=True)
    return jnp.sum(pieces.astype(jnp.float32), axis=0)


def gather_rows(rows):
    groups = lax.axis_size("tensor")
    spread = jnp.broadcast_to(rows[None], (groups,) + rows.shape)
    return lax.all_to_all(spread, "tensor", 0, 0, tiled=True).reshape(-1, rows.shape[1])


HEAD = D // H
INTERPRET = False
CHUNK = 4


def attention_kernel(list_ref, count_ref, q_ref, qid_ref, kt_ref, v_ref, kid_ref, o_ref, m_ref, l_ref, acc_ref):
    i = pl.program_id(0)
    pages = kt_ref.shape[0]
    page = kt_ref.shape[2]
    heads = q_ref.shape[1] // HEAD
    scale = 1.0 / math.sqrt(HEAD)
    q = q_ref[...]
    lane_head = lax.broadcasted_iota(jnp.int32, q.shape, 1) // HEAD
    head_q = [jnp.where(lane_head == h, q, jnp.zeros_like(q)) for h in range(heads)]
    qid = qid_ref[...]
    count = count_ref[i]
    m_ref[...] = jnp.full(m_ref.shape, -1e30, jnp.float32)
    l_ref[...] = jnp.zeros(l_ref.shape, jnp.float32)
    acc_ref[...] = jnp.zeros(acc_ref.shape, jnp.float32)
    slot_chunk = lax.broadcasted_iota(jnp.int32, (1, CHUNK * page), 1) // page

    def body(c, carry):
        base = c * CHUNK
        kps = [list_ref[i * (pages + CHUNK) + base + j] for j in range(CHUNK)]
        kt = jnp.concatenate([kt_ref[kp] for kp in kps], axis=1)
        v = jnp.concatenate([v_ref[kp] for kp in kps], axis=0)
        kid = jnp.concatenate([kid_ref[kp] for kp in kps], axis=1)
        allowed = jnp.logical_and(qid == kid, slot_chunk + base < count)
        for h in range(heads):
            s = jnp.dot(head_q[h], kt, preferred_element_type=jnp.float32) * scale
            s = jnp.where(allowed, s, -1e30)
            m_old = m_ref[h]
            m_new = jnp.maximum(m_old, jnp.max(s, axis=1, keepdims=True))
            p = jnp.where(allowed, jnp.exp(s - m_new), 0.0)
            alpha = jnp.exp(m_old - m_new)
            l_ref[h] = alpha * l_ref[h] + jnp.sum(p, axis=1, keepdims=True)
            acc_ref[h] = alpha * acc_ref[h] + jnp.dot(
                p.astype(jnp.bfloat16), v, preferred_element_type=jnp.float32
            )
            m_ref[h] = m_new
        return carry

    lax.fori_loop(0, (count + CHUNK - 1) // CHUNK, body, 0)
    out = acc_ref[0] / l_ref[0]
    for h in range(1, heads):
        out = jnp.where(lane_head == h, acc_ref[h] / l_ref[h], out)
    o_ref[...] = out.astype(o_ref.dtype)


def paged_attention(queries, keys, values, slot_request, dp_rank):
    pages, page = slot_request.shape
    rows, width = queries.shape
    own_pages = rows // page
    heads = width // HEAD
    present = (
        slot_request[:, :, None] == jnp.arange(-1, 4, dtype=jnp.int32)[None, None, :]
    ).any(axis=1).astype(jnp.float32)
    own = lax.dynamic_slice_in_dim(present, dp_rank * own_pages, own_pages, 0)
    allowed = (jnp.dot(own, present.T) > 0).astype(jnp.int32)
    counts = jnp.sum(allowed, axis=1)
    visit = jnp.argsort(1 - allowed, axis=1, stable=True).astype(jnp.int32)
    visit = jnp.pad(visit, ((0, 0), (0, CHUNK)), mode="edge").reshape(-1)
    own_ids = lax.dynamic_slice_in_dim(slot_request, dp_rank * own_pages, own_pages, 0)
    qid = own_ids.reshape(rows, 1)
    kid = slot_request.reshape(pages, 1, page)
    kt3 = jnp.transpose(keys.reshape(pages, page, width), (0, 2, 1))
    v3 = values.reshape(pages, page, width)
    grid_spec = pltpu.PrefetchScalarGridSpec(
        num_scalar_prefetch=2,
        grid=(own_pages,),
        in_specs=[
            pl.BlockSpec((page, width), lambda i, a, n: (i, 0)),
            pl.BlockSpec((page, 1), lambda i, a, n: (i, 0)),
            pl.BlockSpec((pages, width, page), lambda i, a, n: (0, 0, 0)),
            pl.BlockSpec((pages, page, width), lambda i, a, n: (0, 0, 0)),
            pl.BlockSpec((pages, 1, page), lambda i, a, n: (0, 0, 0)),
        ],
        out_specs=pl.BlockSpec((page, width), lambda i, a, n: (i, 0)),
        scratch_shapes=[
            pltpu.VMEM((heads, page, 1), jnp.float32),
            pltpu.VMEM((heads, page, 1), jnp.float32),
            pltpu.VMEM((heads, page, width), jnp.float32),
        ],
    )
    return pl.pallas_call(
        attention_kernel,
        grid_spec=grid_spec,
        out_shape=jax.ShapeDtypeStruct((rows, width), jnp.bfloat16),
        interpret=INTERPRET,
    )(visit, counts, queries, qid, kt3, v3, kid)


def shards(tokens, w_qkv, w_out, w_up, w_down, slot_request):
    groups = lax.axis_size("tensor")
    tensor_rank = lax.axis_index("tensor")
    qkv_block, up_block, down_block, out_full = spread_weights(w_qkv, w_out, w_up, w_down)
    tok_rows = tokens.shape[0]
    piece_rows = tok_rows // groups
    head_size = D // H
    heads_here = qkv_block.shape[1] // (3 * head_size)
    qkv = jnp.dot(tokens, qkv_block, preferred_element_type=jnp.float32).astype(jnp.bfloat16)
    qkv = qkv.reshape(tok_rows, heads_here, 3, head_size)
    queries = qkv[:, :, 0, :]
    key_rows = qkv[:, :, 1, :].reshape(tok_rows, heads_here * head_size)
    value_rows = qkv[:, :, 2, :].reshape(tok_rows, heads_here * head_size)
    slot_ids = slot_request.reshape(-1)
    own_ids = lax.dynamic_slice_in_dim(slot_ids, lax.axis_index("dp") * tok_rows, tok_rows, 0)

    key_piece = lax.all_gather(key_rows, "dp", axis=0, tiled=True)
    value_piece = lax.all_gather(value_rows, "dp", axis=0, tiled=True)
    key_piece, value_piece, up_block, down_block, out_full = lax.optimization_barrier(
        (key_piece, value_piece, up_block, down_block, out_full)
    )
    attn = paged_attention(
        queries.reshape(tok_rows, heads_here * head_size),
        key_piece,
        value_piece,
        slot_request,
        lax.axis_index("dp"),
    )
    my_rows = lax.dynamic_slice_in_dim(tokens, tensor_rank * piece_rows, piece_rows, 0)
    my_ids = lax.dynamic_slice_in_dim(own_ids, tensor_rank * piece_rows, piece_rows, 0)
    heads_rows = lax.all_to_all(attn.reshape(groups, piece_rows, -1), "tensor", 0, 0, tiled=True)
    heads_rows = heads_rows.transpose(1, 0, 2).reshape(piece_rows, -1)
    proj = jnp.dot(heads_rows, out_full, preferred_element_type=jnp.float32)
    first_rows = layer_norm(my_rows.astype(jnp.float32) + proj).astype(jnp.bfloat16)
    first = gather_rows(first_rows)
    inner = jax.nn.gelu(
        jnp.dot(first, up_block, preferred_element_type=jnp.float32), approximate=False
    ).astype(jnp.bfloat16)
    ffn = sum_scatter(
        jnp.dot(inner, down_block, preferred_element_type=jnp.float32).astype(jnp.bfloat16)
    )
    live = (my_ids >= 0).astype(jnp.float32)[:, None]
    encoded_rows = (layer_norm(first_rows.astype(jnp.float32) + ffn) * live).astype(jnp.bfloat16)
    return gather_rows(encoded_rows)


def solution(mesh):
    in_specs = (
        P("dp", None),
        P(("dp", "tensor"), None),
        P(None, ("dp", "tensor")),
        P(("dp", "tensor"), None),
        P(None, ("dp", "tensor")),
        P(),
    )
    out_specs = P("dp", None)
    return jax.shard_map(shards, mesh=mesh, in_specs=in_specs, out_specs=out_specs, check_vma=False)
```

profile of v0, /device:TPU:34, one launch (start us, length us, event | category | flops | bytes accessed | tf_op | source)
XLA Modules:
  0.0 322.6 jit_solution(16885455026855291115)
XLA Ops:
  8.0 1.5 reshape.122
  11.7 15.3 %all_to_all.32 = bf16[8,2,9728]{2,1,0:T(2,128)(2,1)S(1)} all-to-all(bf16[8,2,9728]{2,1,0:T(2,128)(2,1)S(1)} %reshape.145), channel_id=1, replica_groups=mesh['dp'=16,'tensor'=8] {'tensor'}, dimensions={0} | all-to-all | bytes 622592 | tf_op jit(solution)/shard_map/all_to_all | solution.py:35
  27.4 1.2 reshape.126
  30.4 2.5 reshape.127
  32.8 2.7 copy.92
  35.6 3.6 %reshape_reshape.11 = bf16[65536]{0:T(1024)(128)(2,1)S(1)} reshape(bf16[1024,8,8]{2,1,0:T(8,128)(2,1)} %copy.92) | data formatting | bytes 262144 | tf_op jit(solution)/shard_map/reshape;reshape | solution.py:45
  40.0 22.5 %all_gather.15 = bf16[1024,384]{1,0:T(8,128)(2,1)S(1)} all-gather(bf16[64,384]{1,0:T(8,128)(2,1)S(1)} %reshape.123), channel_id=1, replica_groups=mesh['dp'=16,'tensor'=8] {'dp'}, dimensions={0}, use_global_device_ids=true | all-gather | bytes 835584 | tf_op jit(solution)/shard_map/all_gather | solution.py:43
  65.7 1.5 sort.17
  70.0 6.6 %all-gather.9.cloned.1.call-done = bf16[2097152]{0:T(1024)(128)(2,1)} async-done(((bf16[131072]{0:T(1024)(128)(2,1)}), bf16[2097152]{0:T(1024)(128)(2,1)}) %all-gather.9.cloned.1.call-update) | async-done | bytes 4194320 | tf_op jit(solution)/shard_map/all_gather | solution.py:46
  76.6 4.7 %reshape.142 = bf16[16,131072]{1,0:T(8,128)(2,1)} reshape(bf16[2097152]{0:T(1024)(128)(2,1)} %all-gather.9.cloned.1.call-done) | data formatting | bytes 8388608 | tf_op jit(solution)/shard_map/all_gather | solution.py:46
  81.3 2.2 copy-done
  83.5 1.1 fusion.77
  84.6 2.3 reshape.129
  86.8 1.6 copy.93
  88.5 1.3 reshape.128
  90.5 5.7 %reshape.131 = bf16[16,1024,64]{2,1,0:T(8,128)(2,1)} reshape(bf16[16,65536]{1,0:T(8,128)(2,1)S(1)} %slice-done) | data formatting | bytes 4194304 | tf_op jit(solution)/shard_map/reshape | solution.py:54
  96.2 4.8 %copy.94 = bf16[1024,16,64]{0,2,1:T(8,128)(2,1)} copy(bf16[1024,16,64]{2,0,1:T(8,128)(2,1)} %bitcast.69) | data formatting | bytes 4194304 | tf_op jit(solution)/shard_map/transpose | solution.py:54
  101.0 12.4 %all-gather.5.cloned.1.call-done = bf16[12288,128]{0,1:T(8,128)(2,1)} async-done(((bf16[768,128]{0,1:T(8,128)(2,1)}), bf16[12288,128]{0,1:T(8,128)(2,1)}) %all-gather.5.cloned.1.call-update) | async-done | bytes 3145744 | tf_op jit(solution)/shard_map/all_gather | solution.py:179
  113.4 37.2 %all-gather.7.cloned.1.call-done = bf16[12288,128]{0,1:T(8,128)(2,1)} async-done(((bf16[768,128]{0,1:T(8,128)(2,1)}), bf16[12288,128]{0,1:T(8,128)(2,1)}) %all-gather.7.cloned.1.call-update) | async-done | bytes 3145744 | tf_op jit(solution)/shard_map/all_gather | solution.py:180
  150.6 3.5 %copy.95 = bf16[12288,128]{1,0:T(8,128)(2,1)S(1)} copy(bf16[12288,128]{0,1:T(8,128)(2,1)} %all-gather.5.cloned.1.call-done) | data formatting | bytes 6291456 | tf_op jit(solution)/shard_map/optimization_barrier | solution.py:181
  154.1 2.8 copy.96
  156.9 4.7 %copy.97 = bf16[12288,128]{1,0:T(8,128)(2,1)} copy(bf16[12288,128]{0,1:T(8,128)(2,1)} %all-gather.7.cloned.1.call-done) | data formatting | bytes 6291456 | tf_op jit(solution)/shard_map/optimization_barrier | solution.py:181
  161.6 65.2 %shard_map.64 = bf16[768,128]{1,0:T(8,128)(2,1)} custom-call(s32[600]{0:T(1024)} %reshape.117.list_ref, s32[6]{0:T(128)} %get-tuple-element.24.count_ref, bf16[768,128]{1,0:T(8,128)(2,1)} %copy.98.q_ref, s32[768,1]{1,0:T(8,128)} %bitcast.79, bf16[96,128,128]{2,1,0:T(8,128)(2,1)} %bitcast.70, bf16[96,128,128]{2,1,0:T(8,128)(2,1)} %bitcast.71, ...), custom_call_target="tpu_custom_call" | custom-call | tf_op jit(solution)/shard_map/pallas_call | solution.py:155
  226.7 5.9 %all-to-all-start.1 = ((bf16[8,96,128]{2,1,0:T(8,128)(2,1)}), bf16[8,96,128]{2,1,0:T(8,128)(2,1)S(1)}, u32[]{:S(2)}, u32[]{:S(2)}) async-start(bf16[8,96,128]{2,1,0:T(8,128)(2,1)} %bitcast.84), calls=%async_computation.1 | async-start | bytes 393216 | tf_op jit(solution)/shard_map/all_to_all | solution.py:193
  232.6 8.5 %all-to-all-done.1 = bf16[8,96,128]{2,1,0:T(8,128)(2,1)S(1)} async-done(((bf16[8,96,128]{2,1,0:T(8,128)(2,1)}), bf16[8,96,128]{2,1,0:T(8,128)(2,1)S(1)}, u32[]{:S(2)}, u32[]{:S(2)}) %all-to-all-start.1) | async-done | bytes 196640 | tf_op jit(solution)/shard_map/all_to_all | solution.py:193
  241.1 1.8 fusion.80
  243.5 25.3 %all_to_all.33 = bf16[8,96,1024]{2,1,0:T(8,128)(2,1)S(1)} all-to-all(bf16[8,96,1024]{2,1,0:T(8,128)(2,1)S(1)} %broadcast_in_dim.12), channel_id=1, replica_groups=mesh['dp'=16,'tensor'=8] {'tensor'}, dimensions={0} | all-to-all | bytes 3145728 | tf_op jit(solution)/shard_map/all_to_all | solution.py:68
  268.8 7.3 %convolution_convert_fusion = bf16[768,1024]{1,0:T(8,128)(2,1)} fusion(bf16[512,1024]{0,1:T(8,128)(2,1)S(1)} %bitcast.83, bf16[768,1024]{1,0:T(8,128)(2,1)S(1)} %bitcast.78, bf16[1024,512]{1,0:T(8,128)(2,1)} %reshape.128), kind=kOutput, calls=%fused_computation.2 | convolution fusion | flops 1636958208 | bytes 5242880 | tf_op jit(solution)/shard_map/dot_general | solution.py:202
  276.1 3.6 %all-to-all-start.3 = ((bf16[8,96,1024]{2,1,0:T(8,128)(2,1)}), bf16[8,96,1024]{2,1,0:T(8,128)(2,1)S(1)}, u32[]{:S(2)}, u32[]{:S(2)}) async-start(bf16[8,96,1024]{2,1,0:T(8,128)(2,1)} %bitcast.27), calls=%async_computation.3 | async-start | bytes 3145728 | tf_op jit(solution)/shard_map/all_to_all | solution.py:61
  280.5 15.0 %all-to-all-done.3 = bf16[8,96,1024]{2,1,0:T(8,128)(2,1)S(1)} async-done(((bf16[8,96,1024]{2,1,0:T(8,128)(2,1)}), bf16[8,96,1024]{2,1,0:T(8,128)(2,1)S(1)}, u32[]{:S(2)}, u32[]{:S(2)}) %all-to-all-start.3) | async-done | bytes 1572896 | tf_op jit(solution)/shard_map/all_to_all | solution.py:61
  296.6 18.3 %all_to_all.34 = bf16[8,96,1024]{2,1,0:T(8,128)(2,1)S(1)} all-to-all(bf16[8,96,1024]{2,1,0:T(8,128)(2,1)S(1)} %broadcast_in_dim.13), channel_id=1, replica_groups=mesh['dp'=16,'tensor'=8] {'tensor'}, dimensions={0} | all-to-all | bytes 3145728 | tf_op jit(solution)/shard_map/all_to_all | solution.py:68
  314.9 1.1 copy.121
  (78 shorter events, 15.5 us)
Async XLA Ops:
  6.5 2.9 copy-start.7
  6.5 3.4 %copy-start.5 = (f32[8,4096]{1,0:T(8,128)S(1)}, f32[8,4096]{1,0:T(8,128)}, u32[]{:S(2)}) copy-start(f32[8,4096]{1,0:T(8,128)} %param.9) | copy-start | bytes 393220
  6.5 70.0 %all-gather.9.cloned.1.call-start = ((), (), s32[]{:S(2)}) async-start(), calls=%async_computation.7 | async-start | bytes 4456448 | tf_op jit(solution)/shard_map/all_gather | solution.py:46
  7.5 2.5 copy-start.6
  35.6 26.9 %copy-start.8 = (bf16[768,1024]{1,0:T(8,128)(2,1)S(1)}, bf16[768,1024]{1,0:T(8,128)(2,1)}, u32[]{:S(2)}) copy-start(bf16[768,1024]{1,0:T(8,128)(2,1)} %param.6) | copy-start | bytes 4718596
  39.9 73.5 %all-gather.5.cloned.1.call-start = ((), (), s32[]{:S(2)}) async-start(), calls=%async_computation.5 | async-start | bytes 3342336 | tf_op jit(solution)/shard_map/all_gather | solution.py:179
  62.5 1.9 copy-start.4
  64.2 86.4 %all-gather.7.cloned.1.call-start = ((), (), s32[]{:S(2)}) async-start(), calls=%async_computation.6 | async-start | bytes 3342336 | tf_op jit(solution)/shard_map/all_gather | solution.py:180
  81.3 2.2 copy-start
  86.8 1.6 copy-start.2
  88.5 2.0 slice-start
  161.6 79.5 %copy-start.1 = (bf16[1024,16,64]{0,2,1:T(8,128)(2,1)S(1)}, bf16[1024,16,64]{0,2,1:T(8,128)(2,1)}, u32[]{:S(2)}) copy-start(bf16[1024,16,64]{0,2,1:T(8,128)(2,1)} %copy.94) | copy-start | bytes 6291460
  226.7 14.4 %all-to-all-start.1 = ((bf16[8,96,128]{2,1,0:T(8,128)(2,1)}), bf16[8,96,128]{2,1,0:T(8,128)(2,1)S(1)}, u32[]{:S(2)}, u32[]{:S(2)}) async-start(bf16[8,96,128]{2,1,0:T(8,128)(2,1)} %bitcast.84), calls=%async_computation.1 | async-start | bytes 393216 | tf_op jit(solution)/shard_map/all_to_all | solution.py:193
  243.5 25.3 %copy-start.3 = (bf16[512,16,64]{0,2,1:T(8,128)(2,1)S(1)}, bf16[512,16,64]{0,2,1:T(8,128)(2,1)}, u32[]{:S(2)}) copy-start(bf16[512,16,64]{0,2,1:T(8,128)(2,1)} %copy.93) | copy-start | bytes 3145732
  276.1 19.4 %all-to-all-start.3 = ((bf16[8,96,1024]{2,1,0:T(8,128)(2,1)}), bf16[8,96,1024]{2,1,0:T(8,128)(2,1)S(1)}, u32[]{:S(2)}, u32[]{:S(2)}) async-start(bf16[8,96,1024]{2,1,0:T(8,128)(2,1)} %bitcast.27), calls=%async_computation.3 | async-start | bytes 3145728 | tf_op jit(solution)/shard_map/all_to_all | solution.py:61
Sparse Core Ops, SparseCore 0:
  40.0 36.4 all-gather.8
  78.2 35.1 all-gather.4
  115.1 35.4 all-gather.6
where the time goes:
time: 324 us; the launch traced here: 323 us
  blocking collectives  81.4 us (25%)
  waiting for transfers between devices  79.7 us (25%)
  Pallas kernels  65.2 us (20%)
  local copies, waits for them, and re-layouts  55.7 us (17%)
  between operations  13.5 us (4%)
  matrix products  11 us (3%)
  starting transfers between devices  9.73 us (3%)
  other arithmetic  6.51 us (2%)
    pallas_call x1, Pallas kernels, paged_attention(): pl.pallas_call(attention_kernel, grid_spec=grid_spec, out_shape=jax.Shape...  65.2 us
    all_to_all x2, blocking collectives, gather_rows(): lax.all_to_all(spread, 'tensor', 0, 0, tiled=True)  43.6 us
    all_gather x1, waiting for transfers between devices, shards(): value_piece = lax.all_gather(value_rows, 'dp', axis=0, tiled=True)  37.2 us
    all_gather x1, blocking collectives, spread_weights(): qkv_block = lax.all_gather(qkv_local, 'dp', axis=0, tiled=True)  22.5 us
    all_to_all x1, blocking collectives, spread_weights(): lax.all_to_all(jnp.concatenate(parts, axis=1), 'tensor', 0, 0, tiled=True)  15.3 us
    all_to_all x1, waiting for transfers between devices, sum_scatter(): lax.all_to_all(part.reshape(groups, -1, part.shape[1]), 'tensor', 0, 0, t...  15 us
    all_gather x1, waiting for transfers between devices, shards(): key_piece = lax.all_gather(key_rows, 'dp', axis=0, tiled=True)  12.4 us
    all_to_all x1, waiting for transfers between devices, shards(): lax.all_to_all(attn.reshape(groups, piece_rows, -1), 'tensor', 0, 0, tile...  8.46 us
  transfers between devices with their start and end apart: 5, of which 5 were waited for; matrix products, arithmetic and copies ran while one was open for 9% of the time, Pallas kernels for 0%

commit v1 on v0

--- a/solution.py
+++ b/solution.py
@@ -38,21 +38,15 @@
     qkv_local = piece[0].reshape(groups * rows, -1)
     up_local = piece[1].reshape(groups * rows, -1)
     down_rows = down.shape[0] // groups
-    down_local = piece[2].reshape(groups, down_rows, -1).transpose(1, 0, 2).reshape(down_rows, -1)
-    out_local = piece[3].reshape(groups, out.shape[0], -1).transpose(1, 0, 2).reshape(out.shape[0], -1)
     qkv_block = lax.all_gather(qkv_local, "dp", axis=0, tiled=True)
-    rest = [up_local, down_local, out_local]
+    rest = [up_local, piece[2], piece[3]]
     flat = jnp.concatenate([r.reshape(-1) for r in rest])
     all_flat = lax.all_gather(flat, "dp", axis=0, tiled=False)
     dp_size = all_flat.shape[0]
-    offs = [0, up_local.size, up_local.size + down_local.size, flat.shape[0]]
+    offs = [0, up_local.size, up_local.size + piece[2].size, flat.shape[0]]
     up_block = all_flat[:, offs[0]:offs[1]].reshape(dp_size * up_local.shape[0], -1)
-    down_block = (
-        all_flat[:, offs[1]:offs[2]].reshape(dp_size, *down_local.shape).transpose(1, 0, 2).reshape(down_rows, -1)
-    )
-    out_full = (
-        all_flat[:, offs[2]:offs[3]].reshape(dp_size, *out_local.shape).transpose(1, 0, 2).reshape(out.shape[0], -1)
-    )
+    down_block = all_flat[:, offs[1]:offs[2]].reshape(dp_size, groups, down_rows, -1)
+    out_full = all_flat[:, offs[2]:offs[3]].reshape(dp_size, groups, out.shape[0], -1)
     return qkv_block, up_block, down_block, out_full
 
 
@@ -176,11 +170,14 @@
     slot_ids = slot_request.reshape(-1)
     own_ids = lax.dynamic_slice_in_dim(slot_ids, lax.axis_index("dp") * tok_rows, tok_rows, 0)
 
-    key_piece = lax.all_gather(key_rows, "dp", axis=0, tiled=True)
-    value_piece = lax.all_gather(value_rows, "dp", axis=0, tiled=True)
-    key_piece, value_piece, up_block, down_block, out_full = lax.optimization_barrier(
-        (key_piece, value_piece, up_block, down_block, out_full)
-    )
+    kv_rows = jnp.concatenate([key_rows, value_rows], axis=1)
+    kv_piece = lax.all_gather(kv_rows, "dp", axis=0, tiled=True)
+    kv_piece, up_block, down_block, out_full = lax.optimization_barrier(
+        (kv_piece, up_block, down_block, out_full)
+    )
+    kv_width = key_rows.shape[1]
+    key_piece = kv_piece[:, :kv_width]
+    value_piece = kv_piece[:, kv_width:]
     attn = paged_attention(
         queries.reshape(tok_rows, heads_here * head_size),
         key_piece,
@@ -188,19 +185,20 @@
         slot_request,
         lax.axis_index("dp"),
     )
-    my_rows = lax.dynamic_slice_in_dim(tokens, tensor_rank * piece_rows, piece_rows, 0)
     my_ids = lax.dynamic_slice_in_dim(own_ids, tensor_rank * piece_rows, piece_rows, 0)
-    heads_rows = lax.all_to_all(attn.reshape(groups, piece_rows, -1), "tensor", 0, 0, tiled=True)
-    heads_rows = heads_rows.transpose(1, 0, 2).reshape(piece_rows, -1)
-    proj = jnp.dot(heads_rows, out_full, preferred_element_type=jnp.float32)
-    first_rows = layer_norm(my_rows.astype(jnp.float32) + proj).astype(jnp.bfloat16)
-    first = gather_rows(first_rows)
+    spread = jnp.broadcast_to(attn[None], (groups,) + attn.shape)
+    heads_all = lax.all_to_all(spread, "tensor", 0, 0, tiled=True)
+    out_split = out_full.reshape(out_full.shape[0], groups, groups, -1, out_full.shape[3])
+    proj = jnp.einsum(
+        "tri,dstij->rdsj", heads_all, out_split, preferred_element_type=jnp.float32
+    ).reshape(tok_rows, -1)
+    first = layer_norm(tokens.astype(jnp.float32) + proj).astype(jnp.bfloat16)
     inner = jax.nn.gelu(
         jnp.dot(first, up_block, preferred_element_type=jnp.float32), approximate=False
     ).astype(jnp.bfloat16)
-    ffn = sum_scatter(
-        jnp.dot(inner, down_block, preferred_element_type=jnp.float32).astype(jnp.bfloat16)
-    )
+    partial = jnp.einsum("rk,dtkj->rdtj", inner, down_block, preferred_element_type=jnp.float32)
+    ffn = sum_scatter(partial.reshape(tok_rows, -1).astype(jnp.bfloat16))
+    first_rows = lax.dynamic_slice_in_dim(first, tensor_rank * piece_rows, piece_rows, 0)
     live = (my_ids >= 0).astype(jnp.float32)[:, None]
     encoded_rows = (layer_norm(first_rows.astype(jnp.float32) + ffn) * live).astype(jnp.bfloat16)
     return gather_rows(encoded_rows)

time: 324 us -> 296 us (0.914)
  the two profiles are of different devices: /device:TPU:34 before, /device:TPU:0 now
where the time goes in v1:
time: 296 us; the launch traced here: 295 us
  local copies, waits for them, and re-layouts  81.2 us (27%)
  blocking collectives  61.8 us (21%)
  Pallas kernels  58.4 us (20%)
  waiting for transfers between devices  39.7 us (13%)
  matrix products  16.2 us (5%)
  between operations  13.8 us (5%)
  starting transfers between devices  13.7 us (5%)
  other arithmetic  10.5 us (4%)
    pallas_call x1, Pallas kernels, paged_attention(): pl.pallas_call(attention_kernel, grid_spec=grid_spec, out_shape=jax.Shape...  58.4 us
    all_gather x1, blocking collectives, spread_weights(): qkv_block = lax.all_gather(qkv_local, 'dp', axis=0, tiled=True)  24.4 us
    all_to_all x1, blocking collectives, gather_rows(): lax.all_to_all(spread, 'tensor', 0, 0, tiled=True)  21.1 us
    optimization_barrier x1, local copies, waits for them, and re-layouts, shards(): lax.optimization_barrier((kv_piece, up_block, down_block, out_full))  17.5 us
    all_gather x1, waiting for transfers between devices, shards(): kv_piece = lax.all_gather(kv_rows, 'dp', axis=0, tiled=True)  17.4 us
    all_to_all x1, waiting for transfers between devices, sum_scatter(): lax.all_to_all(part.reshape(groups, -1, part.shape[1]), 'tensor', 0, 0, t...  16.9 us
    all_to_all x1, blocking collectives, spread_weights(): lax.all_to_all(jnp.concatenate(parts, axis=1), 'tensor', 0, 0, tiled=True)  16.3 us
    slice x3, local copies, waits for them, and re-layouts, spread_weights(): all_flat[:, offs[2]:offs[3]].reshape(dp_size, groups, out.shape[0], -1)  11.8 us
  transfers between devices with their start and end apart: 4, of which 3 were waited for; matrix products, arithmetic and copies ran while one was open for 17% of the time, Pallas kernels for 0%

profile of v1, /device:TPU:0, one launch (start us, length us, event | category | flops | bytes accessed | tf_op | source)
XLA Modules:
  0.0 295.3 jit_solution(8974996495639715130)
XLA Ops:
  8.0 1.5 reshape.113
  11.7 16.3 %all_to_all.27 = bf16[8,2,9728]{2,1,0:T(2,128)(2,1)S(1)} all-to-all(bf16[8,2,9728]{2,1,0:T(2,128)(2,1)S(1)} %reshape.133), channel_id=1, replica_groups=mesh['dp'=16,'tensor'=8] {'tensor'}, dimensions={0} | all-to-all | bytes 622592 | tf_op jit(solution)/shard_map/all_to_all | solution.py:35
  29.3 24.4 %all_gather.12 = bf16[1024,384]{1,0:T(8,128)(2,1)S(1)} all-gather(bf16[64,384]{1,0:T(8,128)(2,1)S(1)} %reshape.114), channel_id=1, replica_groups=mesh['dp'=16,'tensor'=8] {'dp'}, dimensions={0}, use_global_device_ids=true | all-gather | bytes 835584 | tf_op jit(solution)/shard_map/all_gather | solution.py:41
  56.8 1.5 sort.17
  61.0 5.3 %all-gather.6.cloned.1.call-done = bf16[2097152]{0:T(1024)(128)(2,1)} async-done(((bf16[131072]{0:T(1024)(128)(2,1)}), bf16[2097152]{0:T(1024)(128)(2,1)}) %all-gather.6.cloned.1.call-update) | async-done | bytes 4194320 | tf_op jit(solution)/shard_map/all_gather | solution.py:44
  66.3 4.7 %reshape.128 = bf16[16,131072]{1,0:T(8,128)(2,1)} reshape(bf16[2097152]{0:T(1024)(128)(2,1)} %all-gather.6.cloned.1.call-done) | data formatting | bytes 8388608 | tf_op jit(solution)/shard_map/all_gather | solution.py:44
  71.1 2.2 copy-done
  73.4 6.2 %copy.103 = bf16[16,32768]{0,1:T(8,128)(2,1)} copy(bf16[16,32768]{1,0:T(8,128)(2,1)S(1)} %get-tuple-element.17) | data formatting | bytes 2097152 | tf_op jit(solution)/shard_map/slice | solution.py:48
  79.6 1.3 reshape.119
  81.6 11.1 %copy.104 = bf16[16,65536]{0,1:T(8,128)(2,1)} copy(bf16[16,65536]{1,0:T(8,128)(2,1)S(1)} %slice-done) | data formatting | bytes 4194304 | tf_op jit(solution)/shard_map/slice | solution.py:49
  92.7 17.4 %all-gather.4.cloned.1.call-done = bf16[12288,256]{0,1:T(8,128)(2,1)} async-done(((bf16[768,256]{0,1:T(8,128)(2,1)}), bf16[12288,256]{0,1:T(8,128)(2,1)}) %all-gather.4.cloned.1.call-update) | async-done | bytes 6291472 | tf_op jit(solution)/shard_map/all_gather | solution.py:174
  110.2 6.2 %fusion.84 = (bf16[12288,128]{0,1:T(8,128)(2,1)}, bf16[12288,128]{0,1:T(8,128)(2,1)}) fusion(bf16[12288,256]{0,1:T(8,128)(2,1)} %all-gather.4.cloned.1.call-done), kind=kLoop, calls=%fused_computation.116 | loop fusion | bytes 12582912 | tf_op jit(solution)/shard_map/slice | solution.py:180
  116.4 3.5 %copy.105 = bf16[12288,128]{1,0:T(8,128)(2,1)S(1)} copy(bf16[12288,128]{0,1:T(8,128)(2,1)} %get-tuple-element.16) | data formatting | bytes 6291456 | tf_op jit(solution)/shard_map/slice | solution.py:179
  119.9 2.8 copy.106
  122.7 4.6 %copy.107 = bf16[12288,128]{1,0:T(8,128)(2,1)} copy(bf16[12288,128]{0,1:T(8,128)(2,1)} %get-tuple-element.15) | data formatting | bytes 6291456 | tf_op jit(solution)/shard_map/slice | solution.py:180
  127.3 58.4 %shard_map.64 = bf16[768,128]{1,0:T(8,128)(2,1)} custom-call(s32[600]{0:T(1024)} %reshape.108.list_ref, s32[6]{0:T(128)} %get-tuple-element.24.count_ref, bf16[768,128]{1,0:T(8,128)(2,1)} %copy.108.q_ref, s32[768,1]{1,0:T(8,128)} %bitcast.80, bf16[96,128,128]{2,1,0:T(8,128)(2,1)} %bitcast.73, bf16[96,128,128]{2,1,0:T(8,128)(2,1)} %bitcast.74, ...), custom_call_target="tpu_custom_call" | custom-call | tf_op jit(solution)/shard_map/pallas_call | solution.py:149
  185.7 2.3 broadcast_in_dim.12
  188.0 6.5 %all-to-all-start.1 = ((bf16[8,768,128]{2,1,0:T(8,128)(2,1)}), bf16[8,768,128]{2,1,0:T(8,128)(2,1)}, u32[]{:S(2)}, u32[]{:S(2)}) async-start(bf16[8,768,128]{2,1,0:T(8,128)(2,1)} %broadcast_in_dim.12), calls=%async_computation.1 | async-start | bytes 3145728 | tf_op jit(solution)/shard_map/all_to_all | solution.py:190
  194.5 17.5 %copy.110 = bf16[16,8,1024,8]{2,3,1,0:T(8,128)(2,1)S(1)} copy(bf16[16,8,1024,8]{0,3,2,1:T(8,128)(2,1)} %bitcast.72) | data formatting | bytes 4194304 | tf_op jit(solution)/shard_map/optimization_barrier | solution.py:175
  212.0 2.1 copy.111
  214.1 4.4 %fusion.88 = (f32[768]{0:T(1024)S(1)}, f32[768,1024]{1,0:T(8,128)S(1)}) fusion(bf16[8,768,128]{2,1,0:T(8,128)(2,1)} %all-to-all-done.1, bf16[1024,128,8]{1,2,0:T(8,128)(2,1)} %bitcast.79, bf16[768,1024]{1,0:T(8,128)(2,1)} %param.6), kind=kOutput, calls=%fused_computation.120 | convolution fusion | flops 1612971264 | bytes 8391680 | tf_op jit(solution)/shard_map/tri,dstij->rdsj/dot_general | solution.py:192
  219.3 10.0 %fusion.6 = bf16[768,16,8,8]{0,1,3,2:T(8,128)(2,1)S(1)} fusion(bf16[16,8,512,8]{0,3,2,1:T(8,128)(2,1)} %bitcast.77, bf16[768,1024]{1,0:T(8,128)(2,1)S(1)} %multiply_convert_fusion, bf16[1024,512]{1,0:T(8,128)(2,1)} %reshape.119), kind=kOutput, calls=%fused_computation.9 | convolution fusion | flops 1636958208 | bytes 5242880 | tf_op jit(solution)/shard_map/rk,dtkj->rdtj/dot_general | solution.py:199
  229.3 1.6 copy.114
  230.9 3.7 %convert_element_type.62 = bf16[8,96,1024]{1,0,2:T(8,128)(2,1)S(1)} reshape(bf16[768,16,8,8]{0,3,2,1:T(8,128)(2,1)} %copy.114) | data formatting | bytes 3145728 | tf_op jit(solution)/shard_map/convert_element_type | solution.py:200
  234.7 2.8 copy.115
  237.4 7.2 %all-to-all-start.2 = ((bf16[8,96,1024]{2,1,0:T(8,128)(2,1)}), bf16[8,96,1024]{2,1,0:T(8,128)(2,1)S(1)}, u32[]{:S(2)}, u32[]{:S(2)}) async-start(bf16[8,96,1024]{2,1,0:T(8,128)(2,1)} %copy.115), calls=%async_computation.2 | async-start | bytes 3145728 | tf_op jit(solution)/shard_map/all_to_all | solution.py:55
  245.4 16.9 %all-to-all-done.2 = bf16[8,96,1024]{2,1,0:T(8,128)(2,1)S(1)} async-done(((bf16[8,96,1024]{2,1,0:T(8,128)(2,1)}), bf16[8,96,1024]{2,1,0:T(8,128)(2,1)S(1)}, u32[]{:S(2)}, u32[]{:S(2)}) %all-to-all-start.2) | async-done | bytes 1572896 | tf_op jit(solution)/shard_map/all_to_all | solution.py:55
  262.6 1.1 fusion.51
  263.7 1.1 multiply_reduce_fusion.1
  264.9 1.1 multiply_convert_fusion.1
  266.2 21.1 %all_to_all.28 = bf16[8,96,1024]{2,1,0:T(8,128)(2,1)S(1)} all-to-all(bf16[8,96,1024]{2,1,0:T(8,128)(2,1)S(1)} %broadcast_in_dim.13), channel_id=1, replica_groups=mesh['dp'=16,'tensor'=8] {'tensor'}, dimensions={0} | all-to-all | bytes 3145728 | tf_op jit(solution)/shard_map/all_to_all | solution.py:62
  287.3 1.1 copy.145
  (71 shorter events, 13.4 us)
Async XLA Ops:
  6.5 2.9 copy-start.5
  6.5 3.4 %copy-start.3 = (f32[8,4096]{1,0:T(8,128)S(1)}, f32[8,4096]{1,0:T(8,128)}, u32[]{:S(2)}) copy-start(f32[8,4096]{1,0:T(8,128)} %param.9) | copy-start | bytes 393220
  6.5 59.8 %all-gather.6.cloned.1.call-start = ((), (), s32[]{:S(2)}) async-start(), calls=%async_computation.5 | async-start | bytes 4456448 | tf_op jit(solution)/shard_map/all_gather | solution.py:44
  7.5 2.5 copy-start.4
  28.3 25.4 %copy-start.6 = (bf16[768,1024]{1,0:T(8,128)(2,1)S(1)}, bf16[768,1024]{1,0:T(8,128)(2,1)}, u32[]{:S(2)}) copy-start(bf16[768,1024]{1,0:T(8,128)(2,1)} %param.6) | copy-start | bytes 4718596
  29.2 81.0 %all-gather.4.cloned.1.call-start = ((), (), s32[]{:S(2)}) async-start(), calls=%async_computation.4 | async-start | bytes 6684672 | tf_op jit(solution)/shard_map/all_gather | solution.py:174
  54.6 0.9 copy-start.2
  71.0 2.2 copy-start
  79.6 2.0 slice-start
  188.0 26.1 %all-to-all-start.1 = ((bf16[8,768,128]{2,1,0:T(8,128)(2,1)}), bf16[8,768,128]{2,1,0:T(8,128)(2,1)}, u32[]{:S(2)}, u32[]{:S(2)}) async-start(bf16[8,768,128]{2,1,0:T(8,128)(2,1)} %broadcast_in_dim.12), calls=%async_computation.1 | async-start | bytes 3145728 | tf_op jit(solution)/shard_map/all_to_all | solution.py:190
  219.3 10.0 %copy-start.1 = (bf16[768,1024]{1,0:T(8,128)(2,1)}, bf16[768,1024]{1,0:T(8,128)(2,1)S(1)}, u32[]{:S(2)}) copy-start(bf16[768,1024]{1,0:T(8,128)(2,1)S(1)} %multiply_convert_fusion) | copy-start | bytes 4718596
  237.4 24.9 %all-to-all-start.2 = ((bf16[8,96,1024]{2,1,0:T(8,128)(2,1)}), bf16[8,96,1024]{2,1,0:T(8,128)(2,1)S(1)}, u32[]{:S(2)}, u32[]{:S(2)}) async-start(bf16[8,96,1024]{2,1,0:T(8,128)(2,1)} %copy.115), calls=%async_computation.2 | async-start | bytes 3145728 | tf_op jit(solution)/shard_map/all_to_all | solution.py:55
Sparse Core Ops, SparseCore 0:
  29.3 36.9 all-gather.5
  68.0 42.1 all-gather.3

commit v2 on v1

--- a/solution.py
+++ b/solution.py
@@ -22,32 +22,34 @@
     groups = lax.axis_size("tensor")
     qkv = w_qkv.astype(jnp.bfloat16)
     up = w_up.astype(jnp.bfloat16)
-    out = w_out.astype(jnp.bfloat16)
-    down = w_down.astype(jnp.bfloat16)
+    out_t = w_out.astype(jnp.bfloat16).T
+    down_t = w_down.astype(jnp.bfloat16).T
     rows = qkv.shape[0]
+    cols = out_t.shape[0]
     parts = [
         qkv.reshape(rows, groups, -1).transpose(1, 0, 2).reshape(groups, -1),
         up.reshape(rows, groups, -1).transpose(1, 0, 2).reshape(groups, -1),
-        down.reshape(groups, -1),
-        jnp.broadcast_to(out.reshape(1, -1), (groups, out.size)),
+        down_t.reshape(cols, groups, -1).transpose(1, 0, 2).reshape(groups, -1),
+        jnp.broadcast_to(out_t.reshape(1, -1), (groups, out_t.size)),
     ]
     sizes = [p.shape[1] for p in parts]
     got = lax.all_to_all(jnp.concatenate(parts, axis=1), "tensor", 0, 0, tiled=True)
     cut = [sum(sizes[:k]) for k in range(5)]
     piece = [got[:, cut[k]:cut[k + 1]] for k in range(4)]
     qkv_local = piece[0].reshape(groups * rows, -1)
-    up_local = piece[1].reshape(groups * rows, -1)
-    down_rows = down.shape[0] // groups
+    width = up.shape[1] // groups
+    up_local = piece[1].reshape(groups * rows, width)
+    down_local = piece[2].reshape(-1, width)
+    out_local = piece[3].reshape(-1, width)
     qkv_block = lax.all_gather(qkv_local, "dp", axis=0, tiled=True)
-    rest = [up_local, piece[2], piece[3]]
-    flat = jnp.concatenate([r.reshape(-1) for r in rest])
-    all_flat = lax.all_gather(flat, "dp", axis=0, tiled=False)
-    dp_size = all_flat.shape[0]
-    offs = [0, up_local.size, up_local.size + piece[2].size, flat.shape[0]]
-    up_block = all_flat[:, offs[0]:offs[1]].reshape(dp_size * up_local.shape[0], -1)
-    down_block = all_flat[:, offs[1]:offs[2]].reshape(dp_size, groups, down_rows, -1)
-    out_full = all_flat[:, offs[2]:offs[3]].reshape(dp_size, groups, out.shape[0], -1)
-    return qkv_block, up_block, down_block, out_full
+    rest = jnp.concatenate([up_local, down_local, out_local], axis=0)
+    all_rest = lax.all_gather(rest, "dp", axis=0, tiled=False)
+    dp_size = all_rest.shape[0]
+    offs = [0, up_local.shape[0], up_local.shape[0] + down_local.shape[0], rest.shape[0]]
+    up_block = all_rest[:, offs[0]:offs[1]].reshape(dp_size * up_local.shape[0], width)
+    down_full = all_rest[:, offs[1]:offs[2]].reshape(dp_size, groups, cols, -1)
+    out_full = all_rest[:, offs[2]:offs[3]].reshape(dp_size, groups, cols, -1)
+    return qkv_block, up_block, down_full, out_full
 
 
 def sum_scatter(part):
@@ -67,11 +69,12 @@
 CHUNK = 4
 
 
-def attention_kernel(list_ref, count_ref, q_ref, qid_ref, kt_ref, v_ref, kid_ref, o_ref, m_ref, l_ref, acc_ref):
+def attention_kernel(list_ref, count_ref, q_ref, qid_ref, kv_ref, kid_ref, o_ref, m_ref, l_ref, acc_ref):
     i = pl.program_id(0)
-    pages = kt_ref.shape[0]
-    page = kt_ref.shape[2]
-    heads = q_ref.shape[1] // HEAD
+    pages = kv_ref.shape[0]
+    page = kv_ref.shape[1]
+    width = q_ref.shape[1]
+    heads = width // HEAD
     scale = 1.0 / math.sqrt(HEAD)
     q = q_ref[...]
     lane_head = lax.broadcasted_iota(jnp.int32, q.shape, 1) // HEAD
@@ -86,12 +89,15 @@
     def body(c, carry):
         base = c * CHUNK
         kps = [list_ref[i * (pages + CHUNK) + base + j] for j in range(CHUNK)]
-        kt = jnp.concatenate([kt_ref[kp] for kp in kps], axis=1)
-        v = jnp.concatenate([v_ref[kp] for kp in kps], axis=0)
+        kv = jnp.concatenate([kv_ref[kp] for kp in kps], axis=0)
+        k = kv[:, :width]
+        v = kv[:, width:]
         kid = jnp.concatenate([kid_ref[kp] for kp in kps], axis=1)
         allowed = jnp.logical_and(qid == kid, slot_chunk + base < count)
         for h in range(heads):
-            s = jnp.dot(head_q[h], kt, preferred_element_type=jnp.float32) * scale
+            s = lax.dot_general(
+                head_q[h], k, (((1,), (1,)), ((), ())), preferred_element_type=jnp.float32
+            ) * scale
             s = jnp.where(allowed, s, -1e30)
             m_old = m_ref[h]
             m_new = jnp.maximum(m_old, jnp.max(s, axis=1, keepdims=True))
@@ -111,7 +117,7 @@
     o_ref[...] = out.astype(o_ref.dtype)
 
 
-def paged_attention(queries, keys, values, slot_request, dp_rank):
+def paged_attention(queries, kv, slot_request, dp_rank):
     pages, page = slot_request.shape
     rows, width = queries.shape
     own_pages = rows // page
@@ -127,16 +133,14 @@
     own_ids = lax.dynamic_slice_in_dim(slot_request, dp_rank * own_pages, own_pages, 0)
     qid = own_ids.reshape(rows, 1)
     kid = slot_request.reshape(pages, 1, page)
-    kt3 = jnp.transpose(keys.reshape(pages, page, width), (0, 2, 1))
-    v3 = values.reshape(pages, page, width)
+    kv3 = kv.reshape(pages, page, 2 * width)
     grid_spec = pltpu.PrefetchScalarGridSpec(
         num_scalar_prefetch=2,
         grid=(own_pages,),
         in_specs=[
             pl.BlockSpec((page, width), lambda i, a, n: (i, 0)),
             pl.BlockSpec((page, 1), lambda i, a, n: (i, 0)),
-            pl.BlockSpec((pages, width, page), lambda i, a, n: (0, 0, 0)),
-            pl.BlockSpec((pages, page, width), lambda i, a, n: (0, 0, 0)),
+            pl.BlockSpec((pages, page, 2 * width), lambda i, a, n: (0, 0, 0)),
             pl.BlockSpec((pages, 1, page), lambda i, a, n: (0, 0, 0)),
         ],
         out_specs=pl.BlockSpec((page, width), lambda i, a, n: (i, 0)),
@@ -151,7 +155,7 @@
         grid_spec=grid_spec,
         out_shape=jax.ShapeDtypeStruct((rows, width), jnp.bfloat16),
         interpret=INTERPRET,
-    )(visit, counts, queries, qid, kt3, v3, kid)
+    )(visit, counts, queries, qid, kv3, kid)
 
 
 def shards(tokens, w_qkv, w_out, w_up, w_down, slot_request):
@@ -171,33 +175,32 @@
     own_ids = lax.dynamic_slice_in_dim(slot_ids, lax.axis_index("dp") * tok_rows, tok_rows, 0)
 
     kv_rows = jnp.concatenate([key_rows, value_rows], axis=1)
-    kv_piece = lax.all_gather(kv_rows, "dp", axis=0, tiled=True)
+    kv_piece = lax.all_gather(kv_rows, "dp", axis=0, tiled=False)
     kv_piece, up_block, down_block, out_full = lax.optimization_barrier(
         (kv_piece, up_block, down_block, out_full)
     )
-    kv_width = key_rows.shape[1]
-    key_piece = kv_piece[:, :kv_width]
-    value_piece = kv_piece[:, kv_width:]
     attn = paged_attention(
         queries.reshape(tok_rows, heads_here * head_size),
-        key_piece,
-        value_piece,
+        kv_piece,
         slot_request,
         lax.axis_index("dp"),
     )
     my_ids = lax.dynamic_slice_in_dim(own_ids, tensor_rank * piece_rows, piece_rows, 0)
     spread = jnp.broadcast_to(attn[None], (groups,) + attn.shape)
-    heads_all = lax.all_to_all(spread, "tensor", 0, 0, tiled=True)
-    out_split = out_full.reshape(out_full.shape[0], groups, groups, -1, out_full.shape[3])
-    proj = jnp.einsum(
-        "tri,dstij->rdsj", heads_all, out_split, preferred_element_type=jnp.float32
-    ).reshape(tok_rows, -1)
+    heads_all = lax.all_to_all(spread, "tensor", 0, 2, tiled=True).reshape(tok_rows, -1)
+    out_cols = out_full.reshape(-1, out_full.shape[3])
+    proj = lax.dot_general(
+        heads_all, out_cols, (((1,), (1,)), ((), ())), preferred_element_type=jnp.float32
+    )
     first = layer_norm(tokens.astype(jnp.float32) + proj).astype(jnp.bfloat16)
     inner = jax.nn.gelu(
         jnp.dot(first, up_block, preferred_element_type=jnp.float32), approximate=False
     ).astype(jnp.bfloat16)
-    partial = jnp.einsum("rk,dtkj->rdtj", inner, down_block, preferred_element_type=jnp.float32)
-    ffn = sum_scatter(partial.reshape(tok_rows, -1).astype(jnp.bfloat16))
+    down_cols = down_block.reshape(-1, down_block.shape[3])
+    partial = lax.dot_general(
+        inner, down_cols, (((1,), (1,)), ((), ())), preferred_element_type=jnp.float32
+    )
+    ffn = sum_scatter(partial.astype(jnp.bfloat16))
     first_rows = lax.dynamic_slice_in_dim(first, tensor_rank * piece_rows, piece_rows, 0)
     live = (my_ids >= 0).astype(jnp.float32)[:, None]
     encoded_rows = (layer_norm(first_rows.astype(jnp.float32) + ffn) * live).astype(jnp.bfloat16)

time: 296 us -> 260 us (0.88)
  local copies, waits for them, and re-layouts: 81.2 us -> 13.7 us
  blocking collectives: 61.8 us -> 87.2 us
  waiting for transfers between devices: 39.7 us -> 57.2 us
  starting transfers between devices: 13.7 us -> 4.22 us
  matrix products: 16.2 us -> 11 us
    slice x8 -> x1, local copies, waits for them, and re-layouts: 32.5 us -> 1.79 us  [spread_weights(): out_full = all_rest[:, offs[2]:offs[3]].reshape(dp_size, groups, cols, -1)]
    all_to_all x0 -> x1, blocking collectives: none -> 28.2 us  [shards(): lax.all_to_all(spread, 'tensor', 0, 2, tiled=True).reshape(tok_rows, -1)]
    all_gather x2, waiting for transfers between devices: 22.7 us -> 42.1 us  [the longest x1 37 us: shards(): kv_piece = lax.all_gather(kv_rows, 'dp', axis=0, tiled=False)]
    optimization_barrier x1 -> x0, local copies, waits for them, and re-layouts: 17.5 us -> none  [shards(): lax.optimization_barrier((kv_piece, up_block, down_block, out_full))]
    convert_element_type x5 -> x0, local copies, waits for them, and re-layouts: 8.75 us -> none  [the longest x3 8.11 us: shards(): ffn = sum_scatter(partial.reshape(tok_rows, -1).astype(jnp.bfloat16))]
    all_to_all x1 -> x0, starting transfers between devices: 6.49 us -> none  [shards(): heads_all = lax.all_to_all(spread, 'tensor', 0, 0, tiled=True)]
    dot_general x2, matrix products: 14.4 us -> 9.25 us  [the longest x1 7.32 us: shards(): lax.dot_general(inner, down_cols, (((1,), (1,)), ((), ())), preferred_ele...]
    all_gather x1 -> x0, local copies, waits for them, and re-layouts: 4.71 us -> none  [spread_weights(): all_flat = lax.all_gather(flat, 'dp', axis=0, tiled=False)]
  transfers between devices with their start and end apart: 4 -> 3, of which waited for: 3 -> 3; matrix products, arithmetic and copies ran while one was open for 17% -> 6% of each run, Pallas kernels for 0% -> 0%
where the time goes in v2:
time: 260 us; the launch traced here: 257 us
  blocking collectives  87.2 us (34%)
  Pallas kernels  59.6 us (23%)
  waiting for transfers between devices  57.2 us (22%)
  local copies, waits for them, and re-layouts  13.7 us (5%)
  between operations  13.7 us (5%)
  matrix products  11 us (4%)
  other arithmetic  10.2 us (4%)
  starting transfers between devices  4.22 us (2%)
    pallas_call x1, Pallas kernels, paged_attention(): pl.pallas_call(attention_kernel, grid_spec=grid_spec, out_shape=jax.Shape...  59.6 us
    all_gather x1, waiting for transfers between devices, shards(): kv_piece = lax.all_gather(kv_rows, 'dp', axis=0, tiled=False)  37 us
    all_to_all x1, blocking collectives, shards(): lax.all_to_all(spread, 'tensor', 0, 2, tiled=True).reshape(tok_rows, -1)  28.2 us
    all_gather x1, blocking collectives, spread_weights(): qkv_block = lax.all_gather(qkv_local, 'dp', axis=0, tiled=True)  24.4 us
    all_to_all x1, blocking collectives, gather_rows(): lax.all_to_all(spread, 'tensor', 0, 0, tiled=True)  18.3 us
    all_to_all x1, blocking collectives, spread_weights(): lax.all_to_all(jnp.concatenate(parts, axis=1), 'tensor', 0, 0, tiled=True)  16.3 us
    all_to_all x1, waiting for transfers between devices, sum_scatter(): lax.all_to_all(part.reshape(groups, -1, part.shape[1]), 'tensor', 0, 0, t...  15.1 us
    dot_general x1, matrix products, shards(): lax.dot_general(inner, down_cols, (((1,), (1,)), ((), ())), preferred_ele...  7.32 us
  transfers between devices with their start and end apart: 3, of which 3 were waited for; matrix products, arithmetic and copies ran while one was open for 6% of the time, Pallas kernels for 0%

profile of v2, /device:TPU:0, one launch (start us, length us, event | category | flops | bytes accessed | tf_op | source)
XLA Modules:
  0.0 256.8 jit_solution(7513692867335284256)
XLA Ops:
  6.5 0.9 convert_element_type.50
  7.5 0.9 convert_element_type.49
  8.4 0.9 convert_element_type.48
  9.3 0.8 convert_bitcast_fusion
  10.2 0.5 broadcast.71
  10.7 0.8 reduce
  11.8 16.3 %all_to_all.37 = bf16[8,2,9728]{2,1,0:T(2,128)(2,1)S(1)} all-to-all(bf16[8,2,9728]{2,1,0:T(2,128)(2,1)S(1)} %reshape.143), channel_id=1, replica_groups=mesh['dp'=16,'tensor'=8] {'tensor'}, dimensions={0} | all-to-all | bytes 622592 | tf_op jit(solution)/shard_map/all_to_all | solution.py:36
  28.7 0.7 pad_maximum_fusion.1
  29.5 24.4 %all_gather.15 = bf16[1024,384]{1,0:T(8,128)(2,1)S(1)} all-gather(bf16[64,384]{1,0:T(8,128)(2,1)S(1)} %reshape.122), channel_id=1, replica_groups=mesh['dp'=16,'tensor'=8] {'dp'}, dimensions={0}, use_global_device_ids=true | all-gather | bytes 835584 | tf_op jit(solution)/shard_map/all_gather | solution.py:44
  53.9 0.9 convolution_convert_fusion.1
  55.2 0.8 pad_maximum_fusion
  56.3 0.9 fusion.77
  57.3 1.5 sort.17
  59.0 0.7 reshape.115.list_ref
  59.7 0.9 copy.57
  60.7 0.8 copy.50.q_ref
  61.5 5.1 %all-gather.7.cloned.1.call-done = bf16[4096,512]{1,0:T(8,128)(2,1)} async-done(((bf16[256,512]{1,0:T(8,128)(2,1)}), bf16[4096,512]{1,0:T(8,128)(2,1)}) %all-gather.7.cloned.1.call-update) | async-done | bytes 4194320 | tf_op jit(solution)/shard_map/all_gather | solution.py:46
  66.6 1.8 slice.57
  68.4 2.2 reshape.130
  70.6 2.8 %slice_bitcast_fusion = (bf16[16,8,8,512]{3,2,1,0:T(8,128)(2,1)S(1)}, bf16[16,64,512]{2,1,0:T(8,128)(2,1)}) fusion(bf16[16,256,512]{2,1,0:T(8,128)(2,1)} %bitcast.70), kind=kLoop, calls=%fused_computation.27 | loop fusion | bytes 4194304 | tf_op jit(solution)/shard_map/reshape | solution.py:50
  73.4 37.0 %all-gather.5.cloned.1.call-done = bf16[12288,256]{1,0:T(8,128)(2,1)} async-done(((bf16[768,256]{1,0:T(8,128)(2,1)}), bf16[12288,256]{1,0:T(8,128)(2,1)}) %all-gather.5.cloned.1.call-update) | async-done | bytes 6291472 | tf_op jit(solution)/shard_map/all_gather | solution.py:178
  110.4 59.6 %shard_map.64 = bf16[768,128]{1,0:T(8,128)(2,1)} custom-call(s32[600]{0:T(1024)} %reshape.115.list_ref, s32[6]{0:T(128)} %get-tuple-element.22.count_ref, bf16[768,128]{1,0:T(8,128)(2,1)} %copy.50.q_ref, s32[768,1]{1,0:T(8,128)} %bitcast.74, bf16[96,128,256]{2,1,0:T(8,128)(2,1)} %bitcast.67, s32[96,1,128]{2,1,0:T(1,128)} %bitcast.88), custom_call_target="tpu_custom_call" | custom-call | tf_op jit(solution)/shard_map/pallas_call | solution.py:153
  170.0 1.1 copy.52
  171.2 28.2 %all_to_all.38 = bf16[8,768,128]{1,2,0:T(8,128)(2,1)S(1)} all-to-all(bf16[8,768,128]{1,2,0:T(8,128)(2,1)S(1)} %broadcast_in_dim.12), channel_id=1, replica_groups=mesh['dp'=16,'tensor'=8] {'tensor'}, dimensions={0} | all-to-all | bytes 3145728 | tf_op jit(solution)/shard_map/all_to_all | solution.py:190
  199.4 1.9 fusion.78
  201.3 0.4 multiply_reduce_fusion
  202.2 7.3 %convolution_convert_fusion = bf16[768,1024]{1,0:T(8,128)(2,1)} fusion(bf16[1024,512]{1,0:T(8,128)(2,1)S(1)} %bitcast.78, bf16[768,1024]{1,0:T(8,128)(2,1)S(1)} %multiply_convert_fusion, bf16[1024,512]{1,0:T(8,128)(2,1)} %bitcast.79), kind=kOutput, calls=%fused_computation.5 | convolution fusion | flops 1636958208 | bytes 5242880 | tf_op jit(solution)/shard_map/dot_general | solution.py:200
  209.5 4.2 %all-to-all-start.2 = ((bf16[8,96,1024]{2,1,0:T(8,128)(2,1)}), bf16[8,96,1024]{2,1,0:T(8,128)(2,1)S(1)}, u32[]{:S(2)}, u32[]{:S(2)}) async-start(bf16[8,96,1024]{2,1,0:T(8,128)(2,1)} %bitcast.72), calls=%async_computation.2 | async-start | bytes 3145728 | tf_op jit(solution)/shard_map/all_to_all | solution.py:57
  213.7 0.8 compare_convert_fusion
  214.4 15.1 %all-to-all-done.2 = bf16[8,96,1024]{2,1,0:T(8,128)(2,1)S(1)} async-done(((bf16[8,96,1024]{2,1,0:T(8,128)(2,1)}), bf16[8,96,1024]{2,1,0:T(8,128)(2,1)S(1)}, u32[]{:S(2)}, u32[]{:S(2)}) %all-to-all-start.2) | async-done | bytes 1572896 | tf_op jit(solution)/shard_map/all_to_all | solution.py:57
  230.6 18.3 %all_to_all.39 = bf16[8,96,1024]{2,1,0:T(8,128)(2,1)S(1)} all-to-all(bf16[8,96,1024]{2,1,0:T(8,128)(2,1)S(1)} %broadcast_in_dim.13), channel_id=1, replica_groups=mesh['dp'=16,'tensor'=8] {'tensor'}, dimensions={0} | all-to-all | bytes 3145728 | tf_op jit(solution)/shard_map/all_to_all | solution.py:64
  248.9 1.1 copy.66
  (52 shorter events, 3.5 us)
Async XLA Ops:
  6.5 60.1 %all-gather.7.cloned.1.call-start = ((), (), s32[]{:S(2)}) async-start(), calls=%async_computation.5 | async-start | bytes 4456448 | tf_op jit(solution)/shard_map/all_gather | solution.py:46
  28.5 25.5 %copy-start.2 = (bf16[768,1024]{1,0:T(8,128)(2,1)S(1)}, bf16[768,1024]{1,0:T(8,128)(2,1)}, u32[]{:S(2)}) copy-start(bf16[768,1024]{1,0:T(8,128)(2,1)} %param.6) | copy-start | bytes 4718596
  29.4 80.9 %all-gather.5.cloned.1.call-start = ((), (), s32[]{:S(2)}) async-start(), calls=%async_computation.4 | async-start | bytes 6684672 | tf_op jit(solution)/shard_map/all_gather | solution.py:178
  54.8 1.2 copy-start.1
  171.1 28.3 %copy-start.3 = (bf16[768,1024]{1,0:T(8,128)(2,1)S(1)}, bf16[768,1024]{1,0:T(8,128)(2,1)}, u32[]{:S(2)}) copy-start(bf16[768,1024]{1,0:T(8,128)(2,1)} %param.6) | copy-start | bytes 4718596
  171.2 28.2 %copy-start = (bf16[16,8,8,1024]{3,2,1,0:T(8,128)(2,1)S(1)}, bf16[16,8,8,1024]{3,2,1,0:T(8,128)(2,1)}, u32[]{:S(2)}) copy-start(bf16[16,8,8,1024]{3,2,1,0:T(8,128)(2,1)} %reshape.130) | copy-start | bytes 6291460
  209.5 20.0 %all-to-all-start.2 = ((bf16[8,96,1024]{2,1,0:T(8,128)(2,1)}), bf16[8,96,1024]{2,1,0:T(8,128)(2,1)S(1)}, u32[]{:S(2)}, u32[]{:S(2)}) async-start(bf16[8,96,1024]{2,1,0:T(8,128)(2,1)} %bitcast.72), calls=%async_computation.2 | async-start | bytes 3145728 | tf_op jit(solution)/shard_map/all_to_all | solution.py:57
Sparse Core Ops, SparseCore 0:
  29.5 37.0 all-gather.6
  68.3 41.9 all-gather.4

commit v3 on v2

--- a/solution.py
+++ b/solution.py
@@ -66,7 +66,7 @@
 
 HEAD = D // H
 INTERPRET = False
-CHUNK = 4
+CHUNK = 16
 
 
 def attention_kernel(list_ref, count_ref, q_ref, qid_ref, kv_ref, kid_ref, o_ref, m_ref, l_ref, acc_ref):
@@ -97,11 +97,11 @@
         for h in range(heads):
             s = lax.dot_general(
                 head_q[h], k, (((1,), (1,)), ((), ())), preferred_element_type=jnp.float32
-            ) * scale
-            s = jnp.where(allowed, s, -1e30)
+            )
+            s = jnp.where(allowed, s * scale, -jnp.inf)
             m_old = m_ref[h]
             m_new = jnp.maximum(m_old, jnp.max(s, axis=1, keepdims=True))
-            p = jnp.where(allowed, jnp.exp(s - m_new), 0.0)
+            p = jnp.exp(s - m_new)
             alpha = jnp.exp(m_old - m_new)
             l_ref[h] = alpha * l_ref[h] + jnp.sum(p, axis=1, keepdims=True)
             acc_ref[h] = alpha * acc_ref[h] + jnp.dot(

time: 260 us -> 240 us (0.923); the launches traced: 257 us -> 240 us
  Pallas kernels: 59.6 us -> 26 us
  blocking collectives: 87.2 us -> 96.5 us
  waiting for transfers between devices: 57.2 us -> 64.9 us
    pallas_call x1, Pallas kernels: 59.6 us -> 26 us  [paged_attention(): pl.pallas_call(attention_kernel, grid_spec=grid_spec, out_shape=jax.Shape...]
    all_to_all x1, waiting for transfers between devices: 15.1 us -> 22.8 us  [sum_scatter(): lax.all_to_all(part.reshape(groups, -1, part.shape[1]), 'tensor', 0, 0, t...]
    all_to_all x1, blocking collectives: 18.3 us -> 25.5 us  [gather_rows(): lax.all_to_all(spread, 'tensor', 0, 0, tiled=True)]
where the time goes in v3:
time: 240 us
  blocking collectives  96.5 us (40%)
  waiting for transfers between devices  64.9 us (27%)
  Pallas kernels  26 us (11%)
  local copies, waits for them, and re-layouts  13.7 us (6%)
  between operations  13.7 us (6%)
  matrix products  11 us (5%)
  other arithmetic  10.2 us (4%)
  starting transfers between devices  3.63 us (2%)
    all_gather x1, waiting for transfers between devices, shards(): kv_piece = lax.all_gather(kv_rows, 'dp', axis=0, tiled=False)  37 us
    all_to_all x1, blocking collectives, shards(): lax.all_to_all(spread, 'tensor', 0, 2, tiled=True).reshape(tok_rows, -1)  30.3 us
    pallas_call x1, Pallas kernels, paged_attention(): pl.pallas_call(attention_kernel, grid_spec=grid_spec, out_shape=jax.Shape...  26 us
    all_to_all x1, blocking collectives, gather_rows(): lax.all_to_all(spread, 'tensor', 0, 0, tiled=True)  25.5 us
    all_gather x1, blocking collectives, spread_weights(): qkv_block = lax.all_gather(qkv_local, 'dp', axis=0, tiled=True)  24.4 us
    all_to_all x1, waiting for transfers between devices, sum_scatter(): lax.all_to_all(part.reshape(groups, -1, part.shape[1]), 'tensor', 0, 0, t...  22.8 us
    all_to_all x1, blocking collectives, spread_weights(): lax.all_to_all(jnp.concatenate(parts, axis=1), 'tensor', 0, 0, tiled=True)  16.3 us
    dot_general x1, matrix products, shards(): lax.dot_general(inner, down_cols, (((1,), (1,)), ((), ())), preferred_ele...  7.32 us
  transfers between devices with their start and end apart: 3, of which 3 were waited for; matrix products, arithmetic and copies ran while one was open for 6% of the time, Pallas kernels for 0%

profile of v3, /device:TPU:0, one launch (start us, length us, event | category | flops | bytes accessed | tf_op | source)
XLA Modules:
  0.0 239.6 jit_solution(17184178534098667409)
XLA Ops:
  6.5 0.9 convert_element_type.50
  7.5 0.9 convert_element_type.49
  8.4 0.9 convert_element_type.48
  9.3 0.8 convert_bitcast_fusion
  10.2 0.5 broadcast.71
  10.7 0.8 reduce
  11.8 16.3 %all_to_all.37 = bf16[8,2,9728]{2,1,0:T(2,128)(2,1)S(1)} all-to-all(bf16[8,2,9728]{2,1,0:T(2,128)(2,1)S(1)} %reshape.143), channel_id=1, replica_groups=mesh['dp'=16,'tensor'=8] {'tensor'}, dimensions={0} | all-to-all | bytes 622592 | tf_op jit(solution)/shard_map/all_to_all | solution.py:36
  28.7 0.7 pad_maximum_fusion.1
  29.5 24.4 %all_gather.15 = bf16[1024,384]{1,0:T(8,128)(2,1)S(1)} all-gather(bf16[64,384]{1,0:T(8,128)(2,1)S(1)} %reshape.122), channel_id=1, replica_groups=mesh['dp'=16,'tensor'=8] {'dp'}, dimensions={0}, use_global_device_ids=true | all-gather | bytes 835584 | tf_op jit(solution)/shard_map/all_gather | solution.py:44
  53.9 0.9 convolution_convert_fusion.1
  55.2 0.8 pad_maximum_fusion
  56.3 0.9 fusion.77
  57.3 1.5 sort.17
  59.0 0.7 reshape.115.list_ref
  59.7 0.9 copy.57
  60.7 0.8 copy.50.q_ref
  61.5 5.1 %all-gather.7.cloned.1.call-done = bf16[4096,512]{1,0:T(8,128)(2,1)} async-done(((bf16[256,512]{1,0:T(8,128)(2,1)}), bf16[4096,512]{1,0:T(8,128)(2,1)}) %all-gather.7.cloned.1.call-update) | async-done | bytes 4194320 | tf_op jit(solution)/shard_map/all_gather | solution.py:46
  66.6 1.8 slice.57
  68.4 2.2 reshape.130
  70.6 2.8 %slice_bitcast_fusion = (bf16[16,8,8,512]{3,2,1,0:T(8,128)(2,1)S(1)}, bf16[16,64,512]{2,1,0:T(8,128)(2,1)}) fusion(bf16[16,256,512]{2,1,0:T(8,128)(2,1)} %bitcast.70), kind=kLoop, calls=%fused_computation.27 | loop fusion | bytes 4194304 | tf_op jit(solution)/shard_map/reshape | solution.py:50
  73.4 37.0 %all-gather.5.cloned.1.call-done = bf16[12288,256]{1,0:T(8,128)(2,1)} async-done(((bf16[768,256]{1,0:T(8,128)(2,1)}), bf16[12288,256]{1,0:T(8,128)(2,1)}) %all-gather.5.cloned.1.call-update) | async-done | bytes 6291472 | tf_op jit(solution)/shard_map/all_gather | solution.py:178
  110.4 26.0 %shard_map.64 = bf16[768,128]{1,0:T(8,128)(2,1)} custom-call(s32[672]{0:T(1024)} %reshape.115.list_ref, s32[6]{0:T(128)} %get-tuple-element.22.count_ref, bf16[768,128]{1,0:T(8,128)(2,1)} %copy.50.q_ref, s32[768,1]{1,0:T(8,128)} %bitcast.74, bf16[96,128,256]{2,1,0:T(8,128)(2,1)} %bitcast.67, s32[96,1,128]{2,1,0:T(1,128)} %bitcast.88), custom_call_target="tpu_custom_call" | custom-call | tf_op jit(solution)/shard_map/pallas_call | solution.py:153
  136.4 1.1 copy.52
  137.6 30.3 %all_to_all.38 = bf16[8,768,128]{1,2,0:T(8,128)(2,1)S(1)} all-to-all(bf16[8,768,128]{1,2,0:T(8,128)(2,1)S(1)} %broadcast_in_dim.12), channel_id=1, replica_groups=mesh['dp'=16,'tensor'=8] {'tensor'}, dimensions={0} | all-to-all | bytes 3145728 | tf_op jit(solution)/shard_map/all_to_all | solution.py:190
  167.9 1.9 fusion.78
  169.8 0.4 multiply_reduce_fusion
  170.7 7.3 %convolution_convert_fusion = bf16[768,1024]{1,0:T(8,128)(2,1)} fusion(bf16[1024,512]{1,0:T(8,128)(2,1)S(1)} %bitcast.78, bf16[768,1024]{1,0:T(8,128)(2,1)S(1)} %multiply_convert_fusion, bf16[1024,512]{1,0:T(8,128)(2,1)} %bitcast.79), kind=kOutput, calls=%fused_computation.5 | convolution fusion | flops 1636958208 | bytes 5242880 | tf_op jit(solution)/shard_map/dot_general | solution.py:200
  178.0 3.6 %all-to-all-start.2 = ((bf16[8,96,1024]{2,1,0:T(8,128)(2,1)}), bf16[8,96,1024]{2,1,0:T(8,128)(2,1)S(1)}, u32[]{:S(2)}, u32[]{:S(2)}) async-start(bf16[8,96,1024]{2,1,0:T(8,128)(2,1)} %bitcast.72), calls=%async_computation.2 | async-start | bytes 3145728 | tf_op jit(solution)/shard_map/all_to_all | solution.py:57
  181.6 0.8 compare_convert_fusion
  182.4 22.8 %all-to-all-done.2 = bf16[8,96,1024]{2,1,0:T(8,128)(2,1)S(1)} async-done(((bf16[8,96,1024]{2,1,0:T(8,128)(2,1)}), bf16[8,96,1024]{2,1,0:T(8,128)(2,1)S(1)}, u32[]{:S(2)}, u32[]{:S(2)}) %all-to-all-start.2) | async-done | bytes 1572896 | tf_op jit(solution)/shard_map/all_to_all | solution.py:57
  206.2 25.5 %all_to_all.39 = bf16[8,96,1024]{2,1,0:T(8,128)(2,1)S(1)} all-to-all(bf16[8,96,1024]{2,1,0:T(8,128)(2,1)S(1)} %broadcast_in_dim.13), channel_id=1, replica_groups=mesh['dp'=16,'tensor'=8] {'tensor'}, dimensions={0} | all-to-all | bytes 3145728 | tf_op jit(solution)/shard_map/all_to_all | solution.py:64
  231.7 1.1 copy.66
  (52 shorter events, 3.5 us)
Async XLA Ops:
  6.5 60.1 %all-gather.7.cloned.1.call-start = ((), (), s32[]{:S(2)}) async-start(), calls=%async_computation.5 | async-start | bytes 4456448 | tf_op jit(solution)/shard_map/all_gather | solution.py:46
  28.5 25.5 %copy-start.2 = (bf16[768,1024]{1,0:T(8,128)(2,1)S(1)}, bf16[768,1024]{1,0:T(8,128)(2,1)}, u32[]{:S(2)}) copy-start(bf16[768,1024]{1,0:T(8,128)(2,1)} %param.6) | copy-start | bytes 4718596
  29.4 80.9 %all-gather.5.cloned.1.call-start = ((), (), s32[]{:S(2)}) async-start(), calls=%async_computation.4 | async-start | bytes 6684672 | tf_op jit(solution)/shard_map/all_gather | solution.py:178
  54.8 1.2 copy-start.1
  137.4 30.5 %copy-start.3 = (bf16[768,1024]{1,0:T(8,128)(2,1)S(1)}, bf16[768,1024]{1,0:T(8,128)(2,1)}, u32[]{:S(2)}) copy-start(bf16[768,1024]{1,0:T(8,128)(2,1)} %param.6) | copy-start | bytes 4718596
  137.6 30.3 %copy-start = (bf16[16,8,8,1024]{3,2,1,0:T(8,128)(2,1)S(1)}, bf16[16,8,8,1024]{3,2,1,0:T(8,128)(2,1)}, u32[]{:S(2)}) copy-start(bf16[16,8,8,1024]{3,2,1,0:T(8,128)(2,1)} %reshape.130) | copy-start | bytes 6291460
  178.0 27.1 %all-to-all-start.2 = ((bf16[8,96,1024]{2,1,0:T(8,128)(2,1)}), bf16[8,96,1024]{2,1,0:T(8,128)(2,1)S(1)}, u32[]{:S(2)}, u32[]{:S(2)}) async-start(bf16[8,96,1024]{2,1,0:T(8,128)(2,1)} %bitcast.72), calls=%async_computation.2 | async-start | bytes 3145728 | tf_op jit(solution)/shard_map/all_to_all | solution.py:57
Sparse Core Ops, SparseCore 0:
  29.5 37.0 all-gather.6
  68.3 41.9 all-gather.4

commit v4 on v3

--- a/solution.py
+++ b/solution.py
@@ -26,22 +26,26 @@
     down_t = w_down.astype(jnp.bfloat16).T
     rows = qkv.shape[0]
     cols = out_t.shape[0]
+    dp_size = lax.axis_size("dp")
+    qkv_parts = qkv.reshape(rows, groups, -1).transpose(1, 0, 2)
+    qkv_send = jnp.broadcast_to(qkv_parts[None], (dp_size,) + qkv_parts.shape)
+    qkv_got = lax.all_to_all(
+        qkv_send.reshape((dp_size * groups,) + qkv_parts.shape[1:]), ("dp", "tensor"), 0, 0, tiled=True
+    )
+    qkv_block = qkv_got.reshape(-1, qkv_parts.shape[2])
     parts = [
-        qkv.reshape(rows, groups, -1).transpose(1, 0, 2).reshape(groups, -1),
         up.reshape(rows, groups, -1).transpose(1, 0, 2).reshape(groups, -1),
         down_t.reshape(cols, groups, -1).transpose(1, 0, 2).reshape(groups, -1),
         jnp.broadcast_to(out_t.reshape(1, -1), (groups, out_t.size)),
     ]
     sizes = [p.shape[1] for p in parts]
     got = lax.all_to_all(jnp.concatenate(parts, axis=1), "tensor", 0, 0, tiled=True)
-    cut = [sum(sizes[:k]) for k in range(5)]
-    piece = [got[:, cut[k]:cut[k + 1]] for k in range(4)]
-    qkv_local = piece[0].reshape(groups * rows, -1)
+    cut = [sum(sizes[:k]) for k in range(4)]
+    piece = [got[:, cut[k]:cut[k + 1]] for k in range(3)]
     width = up.shape[1] // groups
-    up_local = piece[1].reshape(groups * rows, width)
-    down_local = piece[2].reshape(-1, width)
-    out_local = piece[3].reshape(-1, width)
-    qkv_block = lax.all_gather(qkv_local, "dp", axis=0, tiled=True)
+    up_local = piece[0].reshape(groups * rows, width)
+    down_local = piece[1].reshape(-1, width)
+    out_local = piece[2].reshape(-1, width)
     rest = jnp.concatenate([up_local, down_local, out_local], axis=0)
     all_rest = lax.all_gather(rest, "dp", axis=0, tiled=False)
     dp_size = all_rest.shape[0]

time: 240 us -> 240 us (level)
  Pallas kernels: 26 us -> 20.1 us
  waiting for transfers between devices: 64.9 us -> 70.8 us
    all_to_all x0 -> x1, blocking collectives: none -> 25.2 us  [spread_weights(): lax.all_to_all(qkv_send.reshape((dp_size * groups,) + qkv_parts.shape[1:]...]
    all_gather x1 -> x0, blocking collectives: 24.4 us -> none  [spread_weights(): qkv_block = lax.all_gather(qkv_local, 'dp', axis=0, tiled=True)]
    pallas_call x1, Pallas kernels: 26 us -> 20.1 us  [paged_attention(): pl.pallas_call(attention_kernel, grid_spec=grid_spec, out_shape=jax.Shape...]
    all_gather x1, waiting for transfers between devices: 5.13 us -> 10.6 us  [spread_weights(): all_rest = lax.all_gather(rest, 'dp', axis=0, tiled=False)]
where the time goes in v4:
time: 240 us; the launch traced here: 239 us
  blocking collectives  96.6 us (40%)
  waiting for transfers between devices  70.8 us (30%)
  Pallas kernels  20.1 us (8%)
  local copies, waits for them, and re-layouts  13.9 us (6%)
  between operations  13.7 us (6%)
  matrix products  11 us (5%)
  other arithmetic  9.27 us (4%)
  starting transfers between devices  3.63 us (2%)
    all_gather x1, waiting for transfers between devices, shards(): kv_piece = lax.all_gather(kv_rows, 'dp', axis=0, tiled=False)  37.4 us
    all_to_all x1, blocking collectives, shards(): lax.all_to_all(spread, 'tensor', 0, 2, tiled=True).reshape(tok_rows, -1)  30.3 us
    all_to_all x1, blocking collectives, gather_rows(): lax.all_to_all(spread, 'tensor', 0, 0, tiled=True)  25.5 us
    all_to_all x1, blocking collectives, spread_weights(): lax.all_to_all(qkv_send.reshape((dp_size * groups,) + qkv_parts.shape[1:]...  25.2 us
    all_to_all x1, waiting for transfers between devices, sum_scatter(): lax.all_to_all(part.reshape(groups, -1, part.shape[1]), 'tensor', 0, 0, t...  22.8 us
    pallas_call x1, Pallas kernels, paged_attention(): pl.pallas_call(attention_kernel, grid_spec=grid_spec, out_shape=jax.Shape...  20.1 us
    all_to_all x1, blocking collectives, spread_weights(): lax.all_to_all(jnp.concatenate(parts, axis=1), 'tensor', 0, 0, tiled=True)  15.6 us
    all_gather x1, waiting for transfers between devices, spread_weights(): all_rest = lax.all_gather(rest, 'dp', axis=0, tiled=False)  10.6 us
  transfers between devices with their start and end apart: 3, of which 3 were waited for; matrix products, arithmetic and copies ran while one was open for 6% of the time, Pallas kernels for 0%

profile of v4, /device:TPU:0, one launch (start us, length us, event | category | flops | bytes accessed | tf_op | source)
XLA Modules:
  0.0 239.0 jit_solution(1689765549258841254)
XLA Ops:
  6.5 0.9 convert_element_type.47
  7.5 0.9 convert_element_type.48
  8.4 0.8 convert_bitcast_fusion
  9.3 0.5 broadcast.72
  9.8 0.8 reduce
  10.8 15.6 %all_to_all.42 = bf16[8,2,8192]{2,1,0:T(2,128)(2,1)S(1)} all-to-all(bf16[8,2,8192]{2,1,0:T(2,128)(2,1)S(1)} %reshape.144), channel_id=1, replica_groups=mesh['dp'=16,'tensor'=8] {'tensor'}, dimensions={0} | all-to-all | bytes 524288 | tf_op jit(solution)/shard_map/all_to_all | solution.py:42
  27.2 0.7 pad_maximum_fusion.1
  28.1 25.2 %all_to_all.43 = bf16[128,8,384]{2,1,0:T(8,128)(2,1)S(1)} all-to-all(bf16[128,8,384]{2,1,0:T(8,128)(2,1)S(1)} %bitcast.71), channel_id=1, replica_groups=mesh['dp'=16,'tensor'=8] {'dp','tensor'}, dimensions={0} | all-to-all | bytes 1572864 | tf_op jit(solution)/shard_map/all_to_all | solution.py:32
  53.3 0.8 convolution_convert_fusion.1
  54.6 0.8 pad_maximum_fusion
  55.7 0.9 fusion.78
  56.7 1.5 sort.17
  58.4 0.7 reshape.116.list_ref
  59.1 0.9 copy.53
  60.0 0.8 copy.47.q_ref
  60.8 10.6 %all-gather.7.cloned.1.call-done = bf16[4096,512]{1,0:T(8,128)(2,1)} async-done(((bf16[256,512]{1,0:T(8,128)(2,1)}), bf16[4096,512]{1,0:T(8,128)(2,1)}) %all-gather.7.cloned.1.call-update) | async-done | bytes 4194320 | tf_op jit(solution)/shard_map/all_gather | solution.py:50
  71.5 1.8 slice.52
  73.3 2.2 reshape.131
  75.5 2.8 %slice_bitcast_fusion = (bf16[16,8,8,512]{3,2,1,0:T(8,128)(2,1)S(1)}, bf16[16,64,512]{2,1,0:T(8,128)(2,1)}) fusion(bf16[16,256,512]{2,1,0:T(8,128)(2,1)} %bitcast.70), kind=kLoop, calls=%fused_computation.27 | loop fusion | bytes 4194304 | tf_op jit(solution)/shard_map/reshape | solution.py:54
  78.2 37.4 %all-gather.5.cloned.1.call-done = bf16[12288,256]{1,0:T(8,128)(2,1)} async-done(((bf16[768,256]{1,0:T(8,128)(2,1)}), bf16[12288,256]{1,0:T(8,128)(2,1)}) %all-gather.5.cloned.1.call-update) | async-done | bytes 6291472 | tf_op jit(solution)/shard_map/all_gather | solution.py:182
  115.6 20.1 %shard_map.64 = bf16[768,128]{1,0:T(8,128)(2,1)} custom-call(s32[672]{0:T(1024)} %reshape.116.list_ref, s32[6]{0:T(128)} %get-tuple-element.22.count_ref, bf16[768,128]{1,0:T(8,128)(2,1)} %copy.47.q_ref, s32[768,1]{1,0:T(8,128)} %bitcast.75, bf16[96,128,256]{2,1,0:T(8,128)(2,1)} %bitcast.67, s32[96,1,128]{2,1,0:T(1,128)} %bitcast.88), custom_call_target="tpu_custom_call" | custom-call | tf_op jit(solution)/shard_map/pallas_call | solution.py:157
  135.7 1.1 copy.49
  136.9 30.3 %all_to_all.44 = bf16[8,768,128]{1,2,0:T(8,128)(2,1)S(1)} all-to-all(bf16[8,768,128]{1,2,0:T(8,128)(2,1)S(1)} %broadcast_in_dim.15), channel_id=1, replica_groups=mesh['dp'=16,'tensor'=8] {'tensor'}, dimensions={0} | all-to-all | bytes 3145728 | tf_op jit(solution)/shard_map/all_to_all | solution.py:194
  167.2 1.9 fusion.79
  169.2 0.4 multiply_reduce_fusion
  169.6 0.4 multiply_convert_fusion
  170.0 7.3 %convolution_convert_fusion = bf16[768,1024]{1,0:T(8,128)(2,1)} fusion(bf16[1024,512]{1,0:T(8,128)(2,1)S(1)} %bitcast.78, bf16[768,1024]{1,0:T(8,128)(2,1)S(1)} %multiply_convert_fusion, bf16[1024,512]{1,0:T(8,128)(2,1)} %bitcast.79), kind=kOutput, calls=%fused_computation.5 | convolution fusion | flops 1636958208 | bytes 5242880 | tf_op jit(solution)/shard_map/dot_general | solution.py:204
  177.3 3.6 %all-to-all-start.3 = ((bf16[8,96,1024]{2,1,0:T(8,128)(2,1)}), bf16[8,96,1024]{2,1,0:T(8,128)(2,1)S(1)}, u32[]{:S(2)}, u32[]{:S(2)}) async-start(bf16[8,96,1024]{2,1,0:T(8,128)(2,1)} %bitcast.73), calls=%async_computation.3 | async-start | bytes 3145728 | tf_op jit(solution)/shard_map/all_to_all | solution.py:61
  180.9 0.8 compare_convert_fusion
  181.7 22.8 %all-to-all-done.3 = bf16[8,96,1024]{2,1,0:T(8,128)(2,1)S(1)} async-done(((bf16[8,96,1024]{2,1,0:T(8,128)(2,1)}), bf16[8,96,1024]{2,1,0:T(8,128)(2,1)S(1)}, u32[]{:S(2)}, u32[]{:S(2)}) %all-to-all-start.3) | async-done | bytes 1572896 | tf_op jit(solution)/shard_map/all_to_all | solution.py:61
  205.5 25.5 %all_to_all.45 = bf16[8,96,1024]{2,1,0:T(8,128)(2,1)S(1)} all-to-all(bf16[8,96,1024]{2,1,0:T(8,128)(2,1)S(1)} %broadcast_in_dim.16), channel_id=1, replica_groups=mesh['dp'=16,'tensor'=8] {'tensor'}, dimensions={0} | all-to-all | bytes 3145728 | tf_op jit(solution)/shard_map/all_to_all | solution.py:68
  231.0 1.1 copy.63
  (52 shorter events, 3.3 us)
Async XLA Ops:
  6.5 64.9 %all-gather.7.cloned.1.call-start = ((), (), s32[]{:S(2)}) async-start(), calls=%async_computation.6 | async-start | bytes 4456448 | tf_op jit(solution)/shard_map/all_gather | solution.py:50
  26.4 1.6 copy-start.2
  27.2 26.1 %copy-start.3 = (bf16[768,1024]{1,0:T(8,128)(2,1)S(1)}, bf16[768,1024]{1,0:T(8,128)(2,1)}, u32[]{:S(2)}) copy-start(bf16[768,1024]{1,0:T(8,128)(2,1)} %param.6) | copy-start | bytes 4718596
  27.9 87.7 %all-gather.5.cloned.1.call-start = ((), (), s32[]{:S(2)}) async-start(), calls=%async_computation.5 | async-start | bytes 6684672 | tf_op jit(solution)/shard_map/all_gather | solution.py:182
  54.2 1.2 copy-start.1
  136.7 30.5 %copy-start.4 = (bf16[768,1024]{1,0:T(8,128)(2,1)S(1)}, bf16[768,1024]{1,0:T(8,128)(2,1)}, u32[]{:S(2)}) copy-start(bf16[768,1024]{1,0:T(8,128)(2,1)} %param.6) | copy-start | bytes 4718596
  136.9 30.3 %copy-start = (bf16[16,8,8,1024]{3,2,1,0:T(8,128)(2,1)S(1)}, bf16[16,8,8,1024]{3,2,1,0:T(8,128)(2,1)}, u32[]{:S(2)}) copy-start(bf16[16,8,8,1024]{3,2,1,0:T(8,128)(2,1)} %reshape.131) | copy-start | bytes 6291460
  177.3 27.1 %all-to-all-start.3 = ((bf16[8,96,1024]{2,1,0:T(8,128)(2,1)}), bf16[8,96,1024]{2,1,0:T(8,128)(2,1)S(1)}, u32[]{:S(2)}, u32[]{:S(2)}) async-start(bf16[8,96,1024]{2,1,0:T(8,128)(2,1)} %bitcast.73), calls=%async_computation.3 | async-start | bytes 3145728 | tf_op jit(solution)/shard_map/all_to_all | solution.py:61
Sparse Core Ops, SparseCore 0:
  28.1 43.3 all-gather.6
  73.2 42.3 all-gather.4

commit v5 on v3

--- a/solution.py
+++ b/solution.py
@@ -1,3 +1,4 @@
+import functools
 import math
 
 import jax
@@ -6,6 +7,7 @@
 from jax.experimental import pallas as pl
 from jax.experimental.pallas import tpu as pltpu
 from jax.sharding import PartitionSpec as P
+
 
 D = 1024
 H = 16
@@ -69,7 +71,13 @@
 CHUNK = 16
 
 
-def attention_kernel(list_ref, count_ref, q_ref, qid_ref, kv_ref, kid_ref, o_ref, m_ref, l_ref, acc_ref):
+def attention_kernel(first, last, list_ref, count_ref, q_ref, qid_ref, kv_ref, kid_ref, *refs):
+    if first:
+        outs = refs[:-3]
+    else:
+        m_in, l_in, acc_in = refs[:3]
+        outs = refs[3:-3]
+    m_ref, l_ref, acc_ref = refs[-3:]
     i = pl.program_id(0)
     pages = kv_ref.shape[0]
     page = kv_ref.shape[1]
@@ -81,9 +89,14 @@
     head_q = [jnp.where(lane_head == h, q, jnp.zeros_like(q)) for h in range(heads)]
     qid = qid_ref[...]
     count = count_ref[i]
-    m_ref[...] = jnp.full(m_ref.shape, -1e30, jnp.float32)
-    l_ref[...] = jnp.zeros(l_ref.shape, jnp.float32)
-    acc_ref[...] = jnp.zeros(acc_ref.shape, jnp.float32)
+    if first:
+        m_ref[...] = jnp.full(m_ref.shape, -1e30, jnp.float32)
+        l_ref[...] = jnp.zeros(l_ref.shape, jnp.float32)
+        acc_ref[...] = jnp.zeros(acc_ref.shape, jnp.float32)
+    else:
+        m_ref[...] = m_in[...]
+        l_ref[...] = l_in[...]
+        acc_ref[...] = acc_in[...]
     slot_chunk = lax.broadcasted_iota(jnp.int32, (1, CHUNK * page), 1) // page
 
     def body(c, carry):
@@ -111,51 +124,88 @@
         return carry
 
     lax.fori_loop(0, (count + CHUNK - 1) // CHUNK, body, 0)
-    out = acc_ref[0] / l_ref[0]
-    for h in range(1, heads):
-        out = jnp.where(lane_head == h, acc_ref[h] / l_ref[h], out)
-    o_ref[...] = out.astype(o_ref.dtype)
-
-
-def paged_attention(queries, kv, slot_request, dp_rank):
-    pages, page = slot_request.shape
+    if last:
+        out = acc_ref[0] / l_ref[0]
+        for h in range(1, heads):
+            out = jnp.where(lane_head == h, acc_ref[h] / l_ref[h], out)
+        outs[0][...] = out.astype(outs[0].dtype)
+    else:
+        outs[0][...] = m_ref[...]
+        outs[1][...] = l_ref[...]
+        outs[2][...] = acc_ref[...]
+
+
+def attention_pass(queries, kv, slot_request, dp_rank, part, parts, state):
+    _, page = slot_request.shape
     rows, width = queries.shape
     own_pages = rows // page
     heads = width // HEAD
+    dp_size = kv.shape[0]
+    part_pages = own_pages // parts
     present = (
         slot_request[:, :, None] == jnp.arange(-1, 4, dtype=jnp.int32)[None, None, :]
     ).any(axis=1).astype(jnp.float32)
     own = lax.dynamic_slice_in_dim(present, dp_rank * own_pages, own_pages, 0)
     allowed = (jnp.dot(own, present.T) > 0).astype(jnp.int32)
+    allowed = allowed.reshape(own_pages, dp_size, own_pages)[:, :, part * part_pages:(part + 1) * part_pages]
+    allowed = allowed.reshape(own_pages, -1)
     counts = jnp.sum(allowed, axis=1)
     visit = jnp.argsort(1 - allowed, axis=1, stable=True).astype(jnp.int32)
     visit = jnp.pad(visit, ((0, 0), (0, CHUNK)), mode="edge").reshape(-1)
     own_ids = lax.dynamic_slice_in_dim(slot_request, dp_rank * own_pages, own_pages, 0)
     qid = own_ids.reshape(rows, 1)
-    kid = slot_request.reshape(pages, 1, page)
-    kv3 = kv.reshape(pages, page, 2 * width)
+    kid = slot_request.reshape(dp_size, own_pages, page)[:, part * part_pages:(part + 1) * part_pages]
+    kid = kid.reshape(-1, 1, page)
+    kv3 = kv.reshape(-1, page, 2 * width)
+    seen = kv3.shape[0]
+    first, last = part == 0, part == parts - 1
+    row_spec = pl.BlockSpec((page, width), lambda i, a, n: (i, 0))
+    state_specs = [
+        pl.BlockSpec((heads, page, 1), lambda i, a, n: (0, i, 0)),
+        pl.BlockSpec((heads, page, 1), lambda i, a, n: (0, i, 0)),
+        pl.BlockSpec((heads, page, width), lambda i, a, n: (0, i, 0)),
+    ]
+    state_shapes = [
+        jax.ShapeDtypeStruct((heads, rows, 1), jnp.float32),
+        jax.ShapeDtypeStruct((heads, rows, 1), jnp.float32),
+        jax.ShapeDtypeStruct((heads, rows, width), jnp.float32),
+    ]
+    in_specs = [
+        row_spec,
+        pl.BlockSpec((page, 1), lambda i, a, n: (i, 0)),
+        pl.BlockSpec((seen, page, 2 * width), lambda i, a, n: (0, 0, 0)),
+        pl.BlockSpec((seen, 1, page), lambda i, a, n: (0, 0, 0)),
+    ]
+    if not first:
+        in_specs = in_specs + state_specs
     grid_spec = pltpu.PrefetchScalarGridSpec(
         num_scalar_prefetch=2,
         grid=(own_pages,),
-        in_specs=[
-            pl.BlockSpec((page, width), lambda i, a, n: (i, 0)),
-            pl.BlockSpec((page, 1), lambda i, a, n: (i, 0)),
-            pl.BlockSpec((pages, page, 2 * width), lambda i, a, n: (0, 0, 0)),
-            pl.BlockSpec((pages, 1, page), lambda i, a, n: (0, 0, 0)),
-        ],
-        out_specs=pl.BlockSpec((page, width), lambda i, a, n: (i, 0)),
+        in_specs=in_specs,
+        out_specs=[row_spec] if last else state_specs,
         scratch_shapes=[
             pltpu.VMEM((heads, page, 1), jnp.float32),
             pltpu.VMEM((heads, page, 1), jnp.float32),
             pltpu.VMEM((heads, page, width), jnp.float32),
         ],
     )
-    return pl.pallas_call(
-        attention_kernel,
+    out_shape = [jax.ShapeDtypeStruct((rows, width), jnp.bfloat16)] if last else state_shapes
+    args = [visit, counts, queries, qid, kv3, kid] + ([] if first else list(state))
+    result = pl.pallas_call(
+        functools.partial(attention_kernel, first, last),
         grid_spec=grid_spec,
-        out_shape=jax.ShapeDtypeStruct((rows, width), jnp.bfloat16),
+        out_shape=out_shape,
         interpret=INTERPRET,
-    )(visit, counts, queries, qid, kv3, kid)
+    )(*args)
+    return result[0] if last else result
+
+
+def paged_attention(queries, kv_parts, slot_request, dp_rank):
+    state = None
+    parts = len(kv_parts)
+    for part, kv in enumerate(kv_parts):
+        state = attention_pass(queries, kv, slot_request, dp_rank, part, parts, state)
+    return state
 
 
 def shards(tokens, w_qkv, w_out, w_up, w_down, slot_request):
@@ -175,13 +225,19 @@
     own_ids = lax.dynamic_slice_in_dim(slot_ids, lax.axis_index("dp") * tok_rows, tok_rows, 0)
 
     kv_rows = jnp.concatenate([key_rows, value_rows], axis=1)
-    kv_piece = lax.all_gather(kv_rows, "dp", axis=0, tiled=False)
-    kv_piece, up_block, down_block, out_full = lax.optimization_barrier(
-        (kv_piece, up_block, down_block, out_full)
-    )
+    kv_rows, up_block, down_block, out_full = lax.optimization_barrier(
+        (kv_rows, up_block, down_block, out_full)
+    )
+    parts = 2
+    part_rows = tok_rows // parts
+    kv_parts = []
+    for p in range(parts):
+        kv_parts.append(
+            lax.all_gather(kv_rows[p * part_rows:(p + 1) * part_rows], "dp", axis=0, tiled=False)
+        )
     attn = paged_attention(
         queries.reshape(tok_rows, heads_here * head_size),
-        kv_piece,
+        kv_parts,
         slot_request,
         lax.axis_index("dp"),
     )
@@ -217,4 +273,5 @@
         P(),
     )
     out_specs = P("dp", None)
+
     return jax.shard_map(shards, mesh=mesh, in_specs=in_specs, out_specs=out_specs, check_vma=False)

time: 240 us -> 273 us (1.14)
  local copies, waits for them, and re-layouts: 13.7 us -> 27.7 us
  waiting for transfers between devices: 64.9 us -> 75.5 us
  Pallas kernels: 26 us -> 32.5 us
    all_gather x0 -> x2, local copies, waits for them, and re-layouts: none -> 9.45 us  [shards(): lax.all_gather(kv_rows[p * part_rows:(p + 1) * part_rows], 'dp', axis=0,...]
    pallas_call x1 -> x2, Pallas kernels: 26 us -> 32.5 us  [attention_pass(): pl.pallas_call(functools.partial(attention_kernel, first, last), grid_spe...]
    all_gather x1, waiting for transfers between devices: 5.13 us -> 11 us  [spread_weights(): all_rest = lax.all_gather(rest, 'dp', axis=0, tiled=False)]
    all_gather x1 -> x2, waiting for transfers between devices: 37 us -> 41.2 us  [shards(): lax.all_gather(kv_rows[p * part_rows:(p + 1) * part_rows], 'dp', axis=0,...]
    reshape x2 -> x8, local copies, waits for them, and re-layouts: 0.76 us -> 3.61 us  [the longest x4 1.48 us: attention_pass(): visit = jnp.pad(visit, ((0, 0), (0, CHUNK)), mode='edge').reshape(-1)]
  transfers between devices with their start and end apart: 3 -> 4, of which waited for: 3 -> 4; matrix products, arithmetic and copies ran while one was open for 6% -> 7% of each run, Pallas kernels for 0% -> 6%
where the time goes in v5:
time: 273 us; the launch traced here: 271 us
  blocking collectives  95.8 us (35%)
  waiting for transfers between devices  75.5 us (28%)
  Pallas kernels  32.5 us (12%)
  local copies, waits for them, and re-layouts  27.7 us (10%)
  between operations  13.4 us (5%)
  other arithmetic  11.7 us (4%)
  matrix products  10.3 us (4%)
  starting transfers between devices  3.67 us (1%)
    all_gather x2, waiting for transfers between devices, shards(): lax.all_gather(kv_rows[p * part_rows:(p + 1) * part_rows], 'dp', axis=0,...  41.2 us
    pallas_call x2, Pallas kernels, attention_pass(): pl.pallas_call(functools.partial(attention_kernel, first, last), grid_spe...  32.5 us
    all_to_all x1, blocking collectives, shards(): lax.all_to_all(spread, 'tensor', 0, 2, tiled=True).reshape(tok_rows, -1)  28.8 us
    all_to_all x1, blocking collectives, gather_rows(): lax.all_to_all(spread, 'tensor', 0, 0, tiled=True)  26.3 us
    all_gather x1, blocking collectives, spread_weights(): qkv_block = lax.all_gather(qkv_local, 'dp', axis=0, tiled=True)  24.4 us
    all_to_all x1, waiting for transfers between devices, sum_scatter(): lax.all_to_all(part.reshape(groups, -1, part.shape[1]), 'tensor', 0, 0, t...  22.6 us
    all_to_all x1, blocking collectives, spread_weights(): lax.all_to_all(jnp.concatenate(parts, axis=1), 'tensor', 0, 0, tiled=True)  16.3 us
    all_gather x1, waiting for transfers between devices, spread_weights(): all_rest = lax.all_gather(rest, 'dp', axis=0, tiled=False)  11 us
  transfers between devices with their start and end apart: 4, of which 4 were waited for; matrix products, arithmetic and copies ran while one was open for 7% of the time, Pallas kernels for 6%

profile of v5, /device:TPU:0, one launch (start us, length us, event | category | flops | bytes accessed | tf_op | source)
XLA Modules:
  0.0 270.6 jit_solution(15263783448901749457)
XLA Ops:
  7.3 0.9 convert_element_type.47
  8.2 0.9 convert_element_type.48
  9.2 0.9 convert_element_type.49
  10.7 0.8 reduce.2
  11.8 16.3 %all_to_all.37 = bf16[8,2,9728]{2,1,0:T(2,128)(2,1)S(1)} all-to-all(bf16[8,2,9728]{2,1,0:T(2,128)(2,1)S(1)} %reshape.187), channel_id=1, replica_groups=mesh['dp'=16,'tensor'=8] {'tensor'}, dimensions={0} | all-to-all | bytes 622592 | tf_op jit(solution)/shard_map/all_to_all | solution.py:38
  29.5 24.4 %all_gather.21 = bf16[1024,384]{1,0:T(8,128)(2,1)S(1)} all-gather(bf16[64,384]{1,0:T(8,128)(2,1)S(1)} %reshape.155), channel_id=1, replica_groups=mesh['dp'=16,'tensor'=8] {'dp'}, dimensions={0}, use_global_device_ids=true | all-gather | bytes 835584 | tf_op jit(solution)/shard_map/all_gather | solution.py:46
  53.9 0.8 convolution_convert_fusion.1
  55.6 11.0 %all-gather.7.cloned.1.call-done = bf16[4096,512]{1,0:T(8,128)(2,1)} async-done(((bf16[256,512]{1,0:T(8,128)(2,1)}), bf16[4096,512]{1,0:T(8,128)(2,1)}) %all-gather.7.cloned.1.call-update) | async-done | bytes 4194320 | tf_op jit(solution)/shard_map/all_gather | solution.py:48
  66.6 1.9 slice.89
  68.5 0.9 copy-done
  69.4 1.2 slice_bitcast_fusion
  70.6 2.2 reshape.163
  75.8 1.1 compare_reduce_fusion
  77.2 0.9 slice_reduce_fusion
  78.4 1.0 sort.31
  80.4 1.0 sort.32
  83.6 1.0 copy.91
  84.5 0.8 copy.81.q_ref
  85.4 24.0 %all-gather.11.cloned.1.call-done = bf16[6144,256]{0,1:T(8,128)(2,1)} async-done(((bf16[384,256]{0,1:T(8,128)(2,1)}), bf16[6144,256]{0,1:T(8,128)(2,1)}) %all-gather.11.cloned.1.call-update) | async-done | bytes 3145744 | tf_op jit(solution)/shard_map/all_gather | solution.py:236
  109.4 4.7 %copy.77 = bf16[6144,256]{1,0:T(8,128)(2,1)} copy(bf16[6144,256]{0,1:T(8,128)(2,1)} %all-gather.11.cloned.1.call-done) | data formatting | bytes 6291456 | tf_op jit(solution)/shard_map/all_gather | solution.py:236
  114.1 16.0 %shard_map.64 = (f32[2,768,1]{2,1,0:T(8,128)}, f32[2,768,1]{2,1,0:T(8,128)}, f32[2,768,128]{2,1,0:T(8,128)}) custom-call(s32[384]{0:T(512)} %reshape.168.list_ref, s32[6]{0:T(128)} %get-tuple-element.23.count_ref, bf16[768,128]{1,0:T(8,128)(2,1)} %copy.81.q_ref, s32[768,1]{1,0:T(8,128)} %bitcast.79, bf16[48,128,256]{2,1,0:T(8,128)(2,1)} %bitcast.75, ...), custom_call_target="tpu_custom_call" | custom-call | tf_op jit(solution)/shard_map/pallas_call | solution.py:194
  130.2 17.1 %all-gather.9.cloned.1.call-done = bf16[6144,256]{0,1:T(8,128)(2,1)} async-done(((bf16[384,256]{0,1:T(8,128)(2,1)}), bf16[6144,256]{0,1:T(8,128)(2,1)}) %all-gather.9.cloned.1.call-update) | async-done | bytes 3145744 | tf_op jit(solution)/shard_map/all_gather | solution.py:236
  147.3 4.7 %copy.74 = bf16[6144,256]{1,0:T(8,128)(2,1)} copy(bf16[6144,256]{0,1:T(8,128)(2,1)} %all-gather.9.cloned.1.call-done) | data formatting | bytes 6291456 | tf_op jit(solution)/shard_map/all_gather | solution.py:236
  152.0 16.5 %shard_map.65 = bf16[768,128]{1,0:T(8,128)(2,1)} custom-call(s32[384]{0:T(512)} %reshape.148.list_ref, s32[6]{0:T(128)} %get-tuple-element.24.count_ref, bf16[768,128]{1,0:T(8,128)(2,1)} %copy.81.q_ref, s32[768,1]{1,0:T(8,128)} %bitcast.80, bf16[48,128,256]{2,1,0:T(8,128)(2,1)} %bitcast.74, s32[48,1,128]{2,1,0:T(1,128)} %bitcast.100, ...), custom_call_target="tpu_custom_call" | custom-call | tf_op jit(solution)/shard_map/pallas_call | solution.py:194
  168.5 1.1 copy.84
  169.7 28.8 %all_to_all.38 = bf16[8,768,128]{1,2,0:T(8,128)(2,1)S(1)} all-to-all(bf16[8,768,128]{1,2,0:T(8,128)(2,1)S(1)} %broadcast_in_dim.13), channel_id=1, replica_groups=mesh['dp'=16,'tensor'=8] {'tensor'}, dimensions={0} | all-to-all | bytes 3145728 | tf_op jit(solution)/shard_map/all_to_all | solution.py:246
  198.5 1.9 fusion.79
  201.3 7.3 %convolution_convert_fusion = bf16[768,1024]{1,0:T(8,128)(2,1)} fusion(bf16[1024,512]{1,0:T(8,128)(2,1)S(1)} %bitcast.87, bf16[768,1024]{1,0:T(8,128)(2,1)S(1)} %multiply_convert_fusion, bf16[1024,512]{1,0:T(8,128)(2,1)} %bitcast.88), kind=kOutput, calls=%fused_computation.5 | convolution fusion | flops 1636958208 | bytes 5242880 | tf_op jit(solution)/shard_map/dot_general | solution.py:256
  208.6 3.6 %all-to-all-start.2 = ((bf16[8,96,1024]{2,1,0:T(8,128)(2,1)}), bf16[8,96,1024]{2,1,0:T(8,128)(2,1)S(1)}, u32[]{:S(2)}, u32[]{:S(2)}) async-start(bf16[8,96,1024]{2,1,0:T(8,128)(2,1)} %bitcast.82), calls=%async_computation.2 | async-start | bytes 3145728 | tf_op jit(solution)/shard_map/all_to_all | solution.py:59
  213.0 22.6 %all-to-all-done.2 = bf16[8,96,1024]{2,1,0:T(8,128)(2,1)S(1)} async-done(((bf16[8,96,1024]{2,1,0:T(8,128)(2,1)}), bf16[8,96,1024]{2,1,0:T(8,128)(2,1)S(1)}, u32[]{:S(2)}, u32[]{:S(2)}) %all-to-all-start.2) | async-done | bytes 1572896 | tf_op jit(solution)/shard_map/all_to_all | solution.py:59
  236.7 26.3 %all_to_all.39 = bf16[8,96,1024]{2,1,0:T(8,128)(2,1)S(1)} all-to-all(bf16[8,96,1024]{2,1,0:T(8,128)(2,1)S(1)} %broadcast_in_dim.14), channel_id=1, replica_groups=mesh['dp'=16,'tensor'=8] {'tensor'}, dimensions={0} | all-to-all | bytes 3145728 | tf_op jit(solution)/shard_map/all_to_all | solution.py:66
  263.0 1.1 copy.100
  (75 shorter events, 13.3 us)
Async XLA Ops:
  6.5 60.0 %all-gather.7.cloned.1.call-start = ((), (), s32[]{:S(2)}) async-start(), calls=%async_computation.4 | async-start | bytes 4456448 | tf_op jit(solution)/shard_map/all_gather | solution.py:48
  28.5 25.5 %copy-start.3 = (bf16[768,1024]{1,0:T(8,128)(2,1)S(1)}, bf16[768,1024]{1,0:T(8,128)(2,1)}, u32[]{:S(2)}) copy-start(bf16[768,1024]{1,0:T(8,128)(2,1)} %param.6) | copy-start | bytes 4718596
  29.4 80.0 %all-gather.11.cloned.1.call-start = ((), (), s32[]{:S(2)}) async-start(), calls=%async_computation.6 | async-start | bytes 3342336 | tf_op jit(solution)/shard_map/all_gather | solution.py:236
  66.6 2.8 %copy-start = (bf16[4096,512]{1,0:T(8,128)(2,1)S(1)}, bf16[4096,512]{1,0:T(8,128)(2,1)}, u32[]{:S(2)}) copy-start(bf16[4096,512]{1,0:T(8,128)(2,1)} %all-gather.7.cloned.1.call-done) | copy-start | bytes 12582916
  72.8 11.8 %copy-start.2 = (bf16[768,2,1,64]{0,3,2,1:T(8,128)(2,1)S(1)}, bf16[768,2,1,64]{0,3,2,1:T(8,128)(2,1)}, u32[]{:S(2)}) copy-start(bf16[768,2,1,64]{0,3,2,1:T(8,128)(2,1)} %get-tuple-element.27) | copy-start | bytes 589828
  73.6 73.7 %all-gather.9.cloned.1.call-start = ((), (), s32[]{:S(2)}) async-start(), calls=%async_computation.5 | async-start | bytes 3342336 | tf_op jit(solution)/shard_map/all_gather | solution.py:236
  169.6 28.9 %copy-start.4 = (bf16[768,1024]{1,0:T(8,128)(2,1)S(1)}, bf16[768,1024]{1,0:T(8,128)(2,1)}, u32[]{:S(2)}) copy-start(bf16[768,1024]{1,0:T(8,128)(2,1)} %param.6) | copy-start | bytes 4718596
  169.7 28.8 %copy-start.1 = (bf16[16,8,8,1024]{3,2,1,0:T(8,128)(2,1)S(1)}, bf16[16,8,8,1024]{3,2,1,0:T(8,128)(2,1)}, u32[]{:S(2)}) copy-start(bf16[16,8,8,1024]{3,2,1,0:T(8,128)(2,1)} %reshape.163) | copy-start | bytes 6291460
  208.6 27.0 %all-to-all-start.2 = ((bf16[8,96,1024]{2,1,0:T(8,128)(2,1)}), bf16[8,96,1024]{2,1,0:T(8,128)(2,1)S(1)}, u32[]{:S(2)}, u32[]{:S(2)}) async-start(bf16[8,96,1024]{2,1,0:T(8,128)(2,1)} %bitcast.82), calls=%async_computation.2 | async-start | bytes 3145728 | tf_op jit(solution)/shard_map/all_to_all | solution.py:59
Sparse Core Ops, SparseCore 0:
  29.5 36.9 all-gather.6
  73.7 35.6 all-gather.10
  111.1 36.1 all-gather.8

commit v6 on v3

--- a/solution.py
+++ b/solution.py
@@ -66,7 +66,7 @@
 
 HEAD = D // H
 INTERPRET = False
-CHUNK = 16
+CHUNK = 24
 
 
 def attention_kernel(list_ref, count_ref, q_ref, qid_ref, kv_ref, kid_ref, o_ref, m_ref, l_ref, acc_ref):
@@ -78,8 +78,11 @@
     scale = 1.0 / math.sqrt(HEAD)
     q = q_ref[...]
     lane_head = lax.broadcasted_iota(jnp.int32, q.shape, 1) // HEAD
-    head_q = [jnp.where(lane_head == h, q, jnp.zeros_like(q)) for h in range(heads)]
+    stacked_q = jnp.concatenate(
+        [jnp.where(lane_head == h, q, jnp.zeros_like(q)) for h in range(heads)], axis=0
+    )
     qid = qid_ref[...]
+    stacked_id = jnp.concatenate([qid] * heads, axis=0)
     count = count_ref[i]
     m_ref[...] = jnp.full(m_ref.shape, -1e30, jnp.float32)
     l_ref[...] = jnp.zeros(l_ref.shape, jnp.float32)
@@ -93,27 +96,29 @@
         k = kv[:, :width]
         v = kv[:, width:]
         kid = jnp.concatenate([kid_ref[kp] for kp in kps], axis=1)
-        allowed = jnp.logical_and(qid == kid, slot_chunk + base < count)
-        for h in range(heads):
-            s = lax.dot_general(
-                head_q[h], k, (((1,), (1,)), ((), ())), preferred_element_type=jnp.float32
-            )
-            s = jnp.where(allowed, s * scale, -jnp.inf)
-            m_old = m_ref[h]
-            m_new = jnp.maximum(m_old, jnp.max(s, axis=1, keepdims=True))
-            p = jnp.exp(s - m_new)
-            alpha = jnp.exp(m_old - m_new)
-            l_ref[h] = alpha * l_ref[h] + jnp.sum(p, axis=1, keepdims=True)
-            acc_ref[h] = alpha * acc_ref[h] + jnp.dot(
-                p.astype(jnp.bfloat16), v, preferred_element_type=jnp.float32
-            )
-            m_ref[h] = m_new
+        allowed = jnp.logical_and(stacked_id == kid, slot_chunk + base < count)
+        s = lax.dot_general(
+            stacked_q, k, (((1,), (1,)), ((), ())), preferred_element_type=jnp.float32
+        )
+        s = jnp.where(allowed, s * scale, -jnp.inf)
+        m_old = m_ref[...]
+        m_new = jnp.maximum(m_old, jnp.max(s, axis=1, keepdims=True))
+        p = jnp.exp(s - m_new)
+        alpha = jnp.exp(m_old - m_new)
+        l_ref[...] = alpha * l_ref[...] + jnp.sum(p, axis=1, keepdims=True)
+        acc_ref[...] = alpha * acc_ref[...] + jnp.dot(
+            p.astype(jnp.bfloat16), v, preferred_element_type=jnp.float32
+        )
+        m_ref[...] = m_new
         return carry
 
     lax.fori_loop(0, (count + CHUNK - 1) // CHUNK, body, 0)
-    out = acc_ref[0] / l_ref[0]
+    rows = q.shape[0]
+    out = acc_ref[0:rows] / l_ref[0:rows]
     for h in range(1, heads):
-        out = jnp.where(lane_head == h, acc_ref[h] / l_ref[h], out)
+        out = jnp.where(
+            lane_head == h, acc_ref[h * rows:(h + 1) * rows] / l_ref[h * rows:(h + 1) * rows], out
+        )
     o_ref[...] = out.astype(o_ref.dtype)
 
 
@@ -145,9 +150,9 @@
         ],
         out_specs=pl.BlockSpec((page, width), lambda i, a, n: (i, 0)),
         scratch_shapes=[
-            pltpu.VMEM((heads, page, 1), jnp.float32),
-            pltpu.VMEM((heads, page, 1), jnp.float32),
-            pltpu.VMEM((heads, page, width), jnp.float32),
+            pltpu.VMEM((heads * page, 1), jnp.float32),
+            pltpu.VMEM((heads * page, 1), jnp.float32),
+            pltpu.VMEM((heads * page, width), jnp.float32),
         ],
     )
     return pl.pallas_call(

time: 240 us -> 233 us (0.971)
  the two profiles are of different devices: /device:TPU:0 before, /device:TPU:2 now
where the time goes in v6:
time: 233 us; the launch traced here: 232 us
  blocking collectives  96.1 us (41%)
  waiting for transfers between devices  62.4 us (27%)
  Pallas kernels  21.9 us (9%)
  local copies, waits for them, and re-layouts  13.7 us (6%)
  between operations  13.7 us (6%)
  matrix products  11 us (5%)
  other arithmetic  10.2 us (4%)
  starting transfers between devices  3.63 us (2%)
    all_gather x1, waiting for transfers between devices, shards(): kv_piece = lax.all_gather(kv_rows, 'dp', axis=0, tiled=False)  37 us
    all_to_all x1, blocking collectives, shards(): lax.all_to_all(spread, 'tensor', 0, 2, tiled=True).reshape(tok_rows, -1)  29.1 us
    all_gather x1, blocking collectives, spread_weights(): qkv_block = lax.all_gather(qkv_local, 'dp', axis=0, tiled=True)  26 us
    all_to_all x1, blocking collectives, gather_rows(): lax.all_to_all(spread, 'tensor', 0, 0, tiled=True)  25.7 us
    pallas_call x1, Pallas kernels, paged_attention(): pl.pallas_call(attention_kernel, grid_spec=grid_spec, out_shape=jax.Shape...  21.9 us
    all_to_all x1, waiting for transfers between devices, sum_scatter(): lax.all_to_all(part.reshape(groups, -1, part.shape[1]), 'tensor', 0, 0, t...  21.2 us
    all_to_all x1, blocking collectives, spread_weights(): lax.all_to_all(jnp.concatenate(parts, axis=1), 'tensor', 0, 0, tiled=True)  15.3 us
    dot_general x1, matrix products, shards(): lax.dot_general(inner, down_cols, (((1,), (1,)), ((), ())), preferred_ele...  7.32 us
  transfers between devices with their start and end apart: 3, of which 3 were waited for; matrix products, arithmetic and copies ran while one was open for 6% of the time, Pallas kernels for 0%

profile of v6, /device:TPU:2, one launch (start us, length us, event | category | flops | bytes accessed | tf_op | source)
XLA Modules:
  0.0 232.5 jit_solution(7996194401827557264)
XLA Ops:
  6.5 0.9 convert_element_type.50
  7.5 0.9 convert_element_type.49
  8.4 0.9 convert_element_type.48
  9.3 0.8 convert_bitcast_fusion
  10.2 0.5 broadcast.71
  10.7 0.8 reduce
  11.8 15.3 %all_to_all.37 = bf16[8,2,9728]{2,1,0:T(2,128)(2,1)S(1)} all-to-all(bf16[8,2,9728]{2,1,0:T(2,128)(2,1)S(1)} %reshape.143), channel_id=1, replica_groups=mesh['dp'=16,'tensor'=8] {'tensor'}, dimensions={0} | all-to-all | bytes 622592 | tf_op jit(solution)/shard_map/all_to_all | solution.py:36
  27.7 0.7 pad_maximum_fusion.1
  28.5 26.0 %all_gather.15 = bf16[1024,384]{1,0:T(8,128)(2,1)S(1)} all-gather(bf16[64,384]{1,0:T(8,128)(2,1)S(1)} %reshape.122), channel_id=1, replica_groups=mesh['dp'=16,'tensor'=8] {'dp'}, dimensions={0}, use_global_device_ids=true | all-gather | bytes 835584 | tf_op jit(solution)/shard_map/all_gather | solution.py:44
  54.5 0.9 convolution_convert_fusion.1
  55.8 0.8 pad_maximum_fusion
  56.9 0.9 fusion.77
  57.9 1.5 sort.17
  59.6 0.7 reshape.115.list_ref
  60.3 0.9 copy.57
  61.3 0.8 copy.50.q_ref
  62.1 4.1 %all-gather.7.cloned.1.call-done = bf16[4096,512]{1,0:T(8,128)(2,1)} async-done(((bf16[256,512]{1,0:T(8,128)(2,1)}), bf16[4096,512]{1,0:T(8,128)(2,1)}) %all-gather.7.cloned.1.call-update) | async-done | bytes 4194320 | tf_op jit(solution)/shard_map/all_gather | solution.py:46
  66.2 1.8 slice.57
  68.0 2.2 reshape.130
  70.1 2.8 %slice_bitcast_fusion = (bf16[16,8,8,512]{3,2,1,0:T(8,128)(2,1)S(1)}, bf16[16,64,512]{2,1,0:T(8,128)(2,1)}) fusion(bf16[16,256,512]{2,1,0:T(8,128)(2,1)} %bitcast.70), kind=kLoop, calls=%fused_computation.27 | loop fusion | bytes 4194304 | tf_op jit(solution)/shard_map/reshape | solution.py:50
  72.9 37.0 %all-gather.5.cloned.1.call-done = bf16[12288,256]{1,0:T(8,128)(2,1)} async-done(((bf16[768,256]{1,0:T(8,128)(2,1)}), bf16[12288,256]{1,0:T(8,128)(2,1)}) %all-gather.5.cloned.1.call-update) | async-done | bytes 6291472 | tf_op jit(solution)/shard_map/all_gather | solution.py:183
  110.0 21.9 %shard_map.64 = bf16[768,128]{1,0:T(8,128)(2,1)} custom-call(s32[720]{0:T(1024)} %reshape.115.list_ref, s32[6]{0:T(128)} %get-tuple-element.22.count_ref, bf16[768,128]{1,0:T(8,128)(2,1)} %copy.50.q_ref, s32[768,1]{1,0:T(8,128)} %bitcast.74, bf16[96,128,256]{2,1,0:T(8,128)(2,1)} %bitcast.67, s32[96,1,128]{2,1,0:T(1,128)} %bitcast.88), custom_call_target="tpu_custom_call" | custom-call | tf_op jit(solution)/shard_map/pallas_call | solution.py:158
  131.8 1.1 copy.52
  133.0 29.1 %all_to_all.38 = bf16[8,768,128]{1,2,0:T(8,128)(2,1)S(1)} all-to-all(bf16[8,768,128]{1,2,0:T(8,128)(2,1)S(1)} %broadcast_in_dim.12), channel_id=1, replica_groups=mesh['dp'=16,'tensor'=8] {'tensor'}, dimensions={0} | all-to-all | bytes 3145728 | tf_op jit(solution)/shard_map/all_to_all | solution.py:195
  162.1 1.9 fusion.78
  164.0 0.4 multiply_reduce_fusion
  164.9 7.3 %convolution_convert_fusion = bf16[768,1024]{1,0:T(8,128)(2,1)} fusion(bf16[1024,512]{1,0:T(8,128)(2,1)S(1)} %bitcast.78, bf16[768,1024]{1,0:T(8,128)(2,1)S(1)} %multiply_convert_fusion, bf16[1024,512]{1,0:T(8,128)(2,1)} %bitcast.79), kind=kOutput, calls=%fused_computation.5 | convolution fusion | flops 1636958208 | bytes 5242880 | tf_op jit(solution)/shard_map/dot_general | solution.py:205
  172.2 3.6 %all-to-all-start.2 = ((bf16[8,96,1024]{2,1,0:T(8,128)(2,1)}), bf16[8,96,1024]{2,1,0:T(8,128)(2,1)S(1)}, u32[]{:S(2)}, u32[]{:S(2)}) async-start(bf16[8,96,1024]{2,1,0:T(8,128)(2,1)} %bitcast.72), calls=%async_computation.2 | async-start | bytes 3145728 | tf_op jit(solution)/shard_map/all_to_all | solution.py:57
  175.8 0.8 compare_convert_fusion
  176.6 21.2 %all-to-all-done.2 = bf16[8,96,1024]{2,1,0:T(8,128)(2,1)S(1)} async-done(((bf16[8,96,1024]{2,1,0:T(8,128)(2,1)}), bf16[8,96,1024]{2,1,0:T(8,128)(2,1)S(1)}, u32[]{:S(2)}, u32[]{:S(2)}) %all-to-all-start.2) | async-done | bytes 1572896 | tf_op jit(solution)/shard_map/all_to_all | solution.py:57
  198.8 25.7 %all_to_all.39 = bf16[8,96,1024]{2,1,0:T(8,128)(2,1)S(1)} all-to-all(bf16[8,96,1024]{2,1,0:T(8,128)(2,1)S(1)} %broadcast_in_dim.13), channel_id=1, replica_groups=mesh['dp'=16,'tensor'=8] {'tensor'}, dimensions={0} | all-to-all | bytes 3145728 | tf_op jit(solution)/shard_map/all_to_all | solution.py:64
  224.5 1.1 copy.66
  (52 shorter events, 3.5 us)
Async XLA Ops:
  6.5 59.6 %all-gather.7.cloned.1.call-start = ((), (), s32[]{:S(2)}) async-start(), calls=%async_computation.5 | async-start | bytes 4456448 | tf_op jit(solution)/shard_map/all_gather | solution.py:46
  27.4 27.1 %copy-start.2 = (bf16[768,1024]{1,0:T(8,128)(2,1)S(1)}, bf16[768,1024]{1,0:T(8,128)(2,1)}, u32[]{:S(2)}) copy-start(bf16[768,1024]{1,0:T(8,128)(2,1)} %param.6) | copy-start | bytes 4718596
  28.4 81.5 %all-gather.5.cloned.1.call-start = ((), (), s32[]{:S(2)}) async-start(), calls=%async_computation.4 | async-start | bytes 6684672 | tf_op jit(solution)/shard_map/all_gather | solution.py:183
  55.4 1.2 copy-start.1
  132.9 29.2 %copy-start.3 = (bf16[768,1024]{1,0:T(8,128)(2,1)S(1)}, bf16[768,1024]{1,0:T(8,128)(2,1)}, u32[]{:S(2)}) copy-start(bf16[768,1024]{1,0:T(8,128)(2,1)} %param.6) | copy-start | bytes 4718596
  133.0 29.1 %copy-start = (bf16[16,8,8,1024]{3,2,1,0:T(8,128)(2,1)S(1)}, bf16[16,8,8,1024]{3,2,1,0:T(8,128)(2,1)}, u32[]{:S(2)}) copy-start(bf16[16,8,8,1024]{3,2,1,0:T(8,128)(2,1)} %reshape.130) | copy-start | bytes 6291460
  172.2 25.6 %all-to-all-start.2 = ((bf16[8,96,1024]{2,1,0:T(8,128)(2,1)}), bf16[8,96,1024]{2,1,0:T(8,128)(2,1)S(1)}, u32[]{:S(2)}, u32[]{:S(2)}) async-start(bf16[8,96,1024]{2,1,0:T(8,128)(2,1)} %bitcast.72), calls=%async_computation.2 | async-start | bytes 3145728 | tf_op jit(solution)/shard_map/all_to_all | solution.py:57
Sparse Core Ops, SparseCore 0:
  28.5 37.5 all-gather.6
  67.9 42.0 all-gather.4

commit v7 on v6

--- a/solution.py
+++ b/solution.py
@@ -181,9 +181,6 @@
 
     kv_rows = jnp.concatenate([key_rows, value_rows], axis=1)
     kv_piece = lax.all_gather(kv_rows, "dp", axis=0, tiled=False)
-    kv_piece, up_block, down_block, out_full = lax.optimization_barrier(
-        (kv_piece, up_block, down_block, out_full)
-    )
     attn = paged_attention(
         queries.reshape(tok_rows, heads_here * head_size),
         kv_piece,

time: 233 us -> 227 us (0.974)
  the two profiles are of different devices: /device:TPU:2 before, /device:TPU:0 now
where the time goes in v7:
time: 227 us; the launch traced here: 228 us
  waiting for transfers between devices  70.1 us (31%)
  blocking collectives  64.3 us (28%)
  local copies, waits for them, and re-layouts  23.2 us (10%)
  Pallas kernels  22 us (10%)
  between operations  13.6 us (6%)
  matrix products  12.9 us (6%)
  starting transfers between devices  11.2 us (5%)
  other arithmetic  10.2 us (4%)
    all_gather x1, waiting for transfers between devices, shards(): kv_piece = lax.all_gather(kv_rows, 'dp', axis=0, tiled=False)  31.6 us
    all_to_all x1, blocking collectives, gather_rows(): lax.all_to_all(spread, 'tensor', 0, 0, tiled=True)  25.7 us
    all_to_all x1, waiting for transfers between devices, sum_scatter(): lax.all_to_all(part.reshape(groups, -1, part.shape[1]), 'tensor', 0, 0, t...  23.4 us
    all_gather x1, blocking collectives, spread_weights(): qkv_block = lax.all_gather(qkv_local, 'dp', axis=0, tiled=True)  22.3 us
    pallas_call x1, Pallas kernels, paged_attention(): pl.pallas_call(attention_kernel, grid_spec=grid_spec, out_shape=jax.Shape...  22 us
    all_to_all x1, blocking collectives, spread_weights(): lax.all_to_all(jnp.concatenate(parts, axis=1), 'tensor', 0, 0, tiled=True)  16.3 us
    all_to_all x1, waiting for transfers between devices, shards(): lax.all_to_all(spread, 'tensor', 0, 2, tiled=True).reshape(tok_rows, -1)  14.6 us
    all_gather x1, local copies, waits for them, and re-layouts, shards(): kv_piece = lax.all_gather(kv_rows, 'dp', axis=0, tiled=False)  8.62 us
  transfers between devices with their start and end apart: 4, of which 4 were waited for; matrix products, arithmetic and copies ran while one was open for 11% of the time, Pallas kernels for 10%

profile of v7, /device:TPU:0, one launch (start us, length us, event | category | flops | bytes accessed | tf_op | source)
XLA Modules:
  0.0 227.5 jit_solution(17059382144376979500)
XLA Ops:
  6.5 0.9 convert_element_type.50
  7.5 0.9 convert_element_type.49
  8.4 0.9 convert_element_type.48
  9.3 0.8 convert_bitcast_fusion
  10.7 0.8 reduce
  11.8 16.3 %all_to_all.37 = bf16[8,2,9728]{2,1,0:T(2,128)(2,1)S(1)} all-to-all(bf16[8,2,9728]{2,1,0:T(2,128)(2,1)S(1)} %reshape.128), channel_id=1, replica_groups=mesh['dp'=16,'tensor'=8] {'tensor'}, dimensions={0} | all-to-all | bytes 622592 | tf_op jit(solution)/shard_map/all_to_all | solution.py:36
  28.5 22.3 %all_gather.15 = bf16[1024,384]{1,0:T(8,128)(2,1)S(1)} all-gather(bf16[64,384]{1,0:T(8,128)(2,1)S(1)} %reshape.110), channel_id=1, replica_groups=mesh['dp'=16,'tensor'=8] {'dp'}, dimensions={0}, use_global_device_ids=true | all-gather | bytes 835584 | tf_op jit(solution)/shard_map/all_gather | solution.py:44
  50.8 0.9 convolution_convert_fusion.1
  51.7 0.8 pad_maximum_fusion
  52.8 0.7 pad_maximum_fusion.1
  53.8 0.9 fusion.78
  54.8 1.5 sort.17
  56.5 0.7 reshape.103.list_ref
  57.2 0.9 copy.63
  58.2 0.8 copy.54.q_ref
  59.0 31.6 %all-gather.5.cloned.1.call-done = bf16[12288,256]{0,1:T(8,128)(2,1)} async-done(((bf16[768,256]{0,1:T(8,128)(2,1)}), bf16[12288,256]{0,1:T(8,128)(2,1)}) %all-gather.5.cloned.1.call-update) | async-done | bytes 6291472 | tf_op jit(solution)/shard_map/all_gather | solution.py:183
  90.5 8.6 %copy.53 = bf16[12288,256]{1,0:T(8,128)(2,1)} copy(bf16[12288,256]{0,1:T(8,128)(2,1)} %all-gather.5.cloned.1.call-done) | data formatting | bytes 12582912 | tf_op jit(solution)/shard_map/all_gather | solution.py:183
  99.2 22.0 %shard_map.64 = bf16[768,128]{1,0:T(8,128)(2,1)} custom-call(s32[720]{0:T(1024)} %reshape.103.list_ref, s32[6]{0:T(128)} %get-tuple-element.14.count_ref, bf16[768,128]{1,0:T(8,128)(2,1)} %copy.54.q_ref, s32[768,1]{1,0:T(8,128)} %bitcast.72, bf16[96,128,256]{2,1,0:T(8,128)(2,1)} %bitcast.67, s32[96,1,128]{2,1,0:T(1,128)} %bitcast.86), custom_call_target="tpu_custom_call" | custom-call | tf_op jit(solution)/shard_map/pallas_call | solution.py:158
  121.2 1.1 copy.56
  122.3 1.2 broadcast_in_dim.12
  123.5 6.3 %all-to-all-start.1 = ((bf16[8,768,128]{1,2,0:T(8,128)(2,1)}), bf16[8,768,128]{1,2,0:T(8,128)(2,1)}, u32[]{:S(2)}, u32[]{:S(2)}) async-start(bf16[8,768,128]{1,2,0:T(8,128)(2,1)} %broadcast_in_dim.12), calls=%async_computation.1 | async-start | bytes 3145728 | tf_op jit(solution)/shard_map/all_to_all | solution.py:192
  130.3 1.8 slice.55
  132.1 2.2 reshape_reshape.6
  134.3 2.8 %fusion.75 = (bf16[16,64,512]{2,1,0:T(8,128)(2,1)S(1)}, bf16[16,64,512]{2,1,0:T(8,128)(2,1)}) fusion(bf16[16,256,512]{2,1,0:T(8,128)(2,1)} %bitcast.70), kind=kLoop, calls=%fused_computation.111 | loop fusion | bytes 4194304 | tf_op jit(solution)/shard_map/slice | solution.py:49
  137.2 14.6 %all-to-all-done.1 = bf16[8,768,128]{1,2,0:T(8,128)(2,1)} async-done(((bf16[8,768,128]{1,2,0:T(8,128)(2,1)}), bf16[8,768,128]{1,2,0:T(8,128)(2,1)}, u32[]{:S(2)}, u32[]{:S(2)}) %all-to-all-start.1) | async-done | bytes 1572896 | tf_op jit(solution)/shard_map/all_to_all | solution.py:192
  151.8 3.8 %fusion.79 = (f32[768]{0:T(1024)S(1)}, f32[768,1024]{1,0:T(8,128)S(1)}) fusion(bf16[768,1024]{0,1:T(8,128)(2,1)} %bitcast.23, bf16[1024,1024]{1,0:T(8,128)(2,1)S(1)} %copy-done, bf16[768,1024]{1,0:T(8,128)(2,1)} %param.6), kind=kOutput, calls=%fused_computation.115 | convolution fusion | flops 1612971264 | bytes 8391680 | tf_op jit(solution)/shard_map/dot_general | solution.py:194
  156.4 7.3 %convolution_convert_fusion = bf16[768,1024]{1,0:T(8,128)(2,1)} fusion(bf16[1024,512]{1,0:T(8,128)(2,1)} %bitcast.77, bf16[768,1024]{1,0:T(8,128)(2,1)S(1)} %multiply_convert_fusion, bf16[1024,512]{1,0:T(8,128)(2,1)S(1)} %bitcast.76), kind=kOutput, calls=%fused_computation.5 | convolution fusion | flops 1636958208 | bytes 5242880 | tf_op jit(solution)/shard_map/dot_general | solution.py:202
  163.8 4.8 %all-to-all-start.2 = ((bf16[8,96,1024]{2,1,0:T(8,128)(2,1)}), bf16[8,96,1024]{2,1,0:T(8,128)(2,1)S(1)}, u32[]{:S(2)}, u32[]{:S(2)}) async-start(bf16[8,96,1024]{2,1,0:T(8,128)(2,1)} %bitcast.71), calls=%async_computation.2 | async-start | bytes 3145728 | tf_op jit(solution)/shard_map/all_to_all | solution.py:57
  168.6 0.8 compare_convert_fusion
  169.4 23.4 %all-to-all-done.2 = bf16[8,96,1024]{2,1,0:T(8,128)(2,1)S(1)} async-done(((bf16[8,96,1024]{2,1,0:T(8,128)(2,1)}), bf16[8,96,1024]{2,1,0:T(8,128)(2,1)S(1)}, u32[]{:S(2)}, u32[]{:S(2)}) %all-to-all-start.2) | async-done | bytes 1572896 | tf_op jit(solution)/shard_map/all_to_all | solution.py:57
  193.8 25.7 %all_to_all.38 = bf16[8,96,1024]{2,1,0:T(8,128)(2,1)S(1)} all-to-all(bf16[8,96,1024]{2,1,0:T(8,128)(2,1)S(1)} %broadcast_in_dim.13), channel_id=1, replica_groups=mesh['dp'=16,'tensor'=8] {'tensor'}, dimensions={0} | all-to-all | bytes 3145728 | tf_op jit(solution)/shard_map/all_to_all | solution.py:64
  219.5 1.1 copy.72
  (50 shorter events, 4.5 us)
Async XLA Ops:
  6.5 84.0 %all-gather.5.cloned.1.call-start = ((), (), s32[]{:S(2)}) async-start(), calls=%async_computation.4 | async-start | bytes 6684672 | tf_op jit(solution)/shard_map/all_gather | solution.py:183
  28.1 22.7 %copy-start.2 = (bf16[768,1024]{1,0:T(8,128)(2,1)S(1)}, bf16[768,1024]{1,0:T(8,128)(2,1)}, u32[]{:S(2)}) copy-start(bf16[768,1024]{1,0:T(8,128)(2,1)} %param.6) | copy-start | bytes 4718596
  51.7 1.8 copy-start.1
  52.5 77.8 %all-gather.7.cloned.1.call-start = ((), (), s32[]{:S(2)}) async-start(), calls=%async_computation.5 | async-start | bytes 4456448 | tf_op jit(solution)/shard_map/all_gather | solution.py:46
  123.5 28.3 %all-to-all-start.1 = ((bf16[8,768,128]{1,2,0:T(8,128)(2,1)}), bf16[8,768,128]{1,2,0:T(8,128)(2,1)}, u32[]{:S(2)}, u32[]{:S(2)}) async-start(bf16[8,768,128]{1,2,0:T(8,128)(2,1)} %broadcast_in_dim.12), calls=%async_computation.1 | async-start | bytes 3145728 | tf_op jit(solution)/shard_map/all_to_all | solution.py:192
  134.3 17.5 %copy-start = (bf16[1024,1024]{1,0:T(8,128)(2,1)S(1)}, bf16[1024,1024]{1,0:T(8,128)(2,1)}, u32[]{:S(2)}) copy-start(bf16[1024,1024]{1,0:T(8,128)(2,1)} %reshape_reshape.6) | copy-start | bytes 6291460
  163.8 29.0 %all-to-all-start.2 = ((bf16[8,96,1024]{2,1,0:T(8,128)(2,1)}), bf16[8,96,1024]{2,1,0:T(8,128)(2,1)S(1)}, u32[]{:S(2)}, u32[]{:S(2)}) async-start(bf16[8,96,1024]{2,1,0:T(8,128)(2,1)} %bitcast.71), calls=%async_computation.2 | async-start | bytes 3145728 | tf_op jit(solution)/shard_map/all_to_all | solution.py:57
Sparse Core Ops, SparseCore 0:
  52.6 37.8 all-gather.4
  92.2 38.0 all-gather.6

commit v8 on v7

--- a/solution.py
+++ b/solution.py
@@ -180,7 +180,7 @@
     own_ids = lax.dynamic_slice_in_dim(slot_ids, lax.axis_index("dp") * tok_rows, tok_rows, 0)
 
     kv_rows = jnp.concatenate([key_rows, value_rows], axis=1)
-    kv_piece = lax.all_gather(kv_rows, "dp", axis=0, tiled=False)
+    kv_piece = lax.optimization_barrier(lax.all_gather(kv_rows, "dp", axis=0, tiled=False))
     attn = paged_attention(
         queries.reshape(tok_rows, heads_here * head_size),
         kv_piece,

time: 227 us -> 220 us (0.969)
  local copies, waits for them, and re-layouts: 23.2 us -> 14.9 us
    all_gather x1, waiting for transfers between devices: 0.5 us -> 13.1 us  [spread_weights(): all_rest = lax.all_gather(rest, 'dp', axis=0, tiled=False)]
    all_gather x1 -> x0, local copies, waits for them, and re-layouts: 8.62 us -> none  [shards(): kv_piece = lax.all_gather(kv_rows, 'dp', axis=0, tiled=False)]
    all_to_all x1, waiting for transfers between devices: 14.6 us -> 6.18 us  [shards(): lax.all_to_all(spread, 'tensor', 0, 2, tiled=True).reshape(tok_rows, -1)]
  transfers between devices with their start and end apart: 4 -> 4, of which waited for: 4 -> 4; matrix products, arithmetic and copies ran while one was open for 11% -> 7% of each run, Pallas kernels for 10% -> 10%
where the time goes in v8:
time: 220 us
  waiting for transfers between devices  72.3 us (33%)
  blocking collectives  64 us (29%)
  Pallas kernels  21.8 us (10%)
  local copies, waits for them, and re-layouts  14.9 us (7%)
  between operations  13.6 us (6%)
  matrix products  13 us (6%)
  other arithmetic  10.2 us (5%)
  starting transfers between devices  10.1 us (5%)
    all_gather x1, waiting for transfers between devices, shards(): lax.all_gather(kv_rows, 'dp', axis=0, tiled=False)  31.5 us
    all_to_all x1, blocking collectives, gather_rows(): lax.all_to_all(spread, 'tensor', 0, 0, tiled=True)  25.5 us
    all_gather x1, blocking collectives, spread_weights(): qkv_block = lax.all_gather(qkv_local, 'dp', axis=0, tiled=True)  22.3 us
    pallas_call x1, Pallas kernels, paged_attention(): pl.pallas_call(attention_kernel, grid_spec=grid_spec, out_shape=jax.Shape...  21.8 us
    all_to_all x1, waiting for transfers between devices, sum_scatter(): lax.all_to_all(part.reshape(groups, -1, part.shape[1]), 'tensor', 0, 0, t...  21.6 us
    all_to_all x1, blocking collectives, spread_weights(): lax.all_to_all(jnp.concatenate(parts, axis=1), 'tensor', 0, 0, tiled=True)  16.3 us
    all_gather x1, waiting for transfers between devices, spread_weights(): all_rest = lax.all_gather(rest, 'dp', axis=0, tiled=False)  13.1 us
    dot_general x1, matrix products, shards(): lax.dot_general(inner, down_cols, (((1,), (1,)), ((), ())), preferred_ele...  7.33 us
  transfers between devices with their start and end apart: 4, of which 4 were waited for; matrix products, arithmetic and copies ran while one was open for 7% of the time, Pallas kernels for 10%

profile of v8, /device:TPU:0, one launch (start us, length us, event | category | flops | bytes accessed | tf_op | source)
XLA Modules:
  0.0 220.1 jit_solution(15758274368112864230)
XLA Ops:
  6.5 0.9 convert_element_type.50
  7.5 0.9 convert_element_type.49
  8.4 0.9 convert_element_type.48
  9.3 0.8 convert_bitcast_fusion
  10.7 0.8 reduce
  11.8 16.3 %all_to_all.37 = bf16[8,2,9728]{2,1,0:T(2,128)(2,1)S(1)} all-to-all(bf16[8,2,9728]{2,1,0:T(2,128)(2,1)S(1)} %reshape.127), channel_id=1, replica_groups=mesh['dp'=16,'tensor'=8] {'tensor'}, dimensions={0} | all-to-all | bytes 622592 | tf_op jit(solution)/shard_map/all_to_all | solution.py:36
  28.5 22.3 %all_gather.15 = bf16[1024,384]{1,0:T(8,128)(2,1)S(1)} all-gather(bf16[64,384]{1,0:T(8,128)(2,1)S(1)} %reshape.110), channel_id=1, replica_groups=mesh['dp'=16,'tensor'=8] {'dp'}, dimensions={0}, use_global_device_ids=true | all-gather | bytes 835584 | tf_op jit(solution)/shard_map/all_gather | solution.py:44
  50.8 0.9 convolution_convert_fusion.1
  52.0 0.8 pad_maximum_fusion
  53.1 0.7 pad_maximum_fusion.1
  54.1 1.0 fusion.78
  55.2 1.5 sort.17
  57.0 0.7 reshape.103.list_ref
  57.7 0.9 copy.57
  58.6 0.8 copy.50.q_ref
  59.4 31.5 %all-gather.5.cloned.1.call-done = bf16[12288,256]{1,0:T(8,128)(2,1)} async-done(((bf16[768,256]{1,0:T(8,128)(2,1)}), bf16[12288,256]{1,0:T(8,128)(2,1)}) %all-gather.5.cloned.1.call-update) | async-done | bytes 6291472 | tf_op jit(solution)/shard_map/all_gather | solution.py:183
  90.9 21.8 %shard_map.64 = bf16[768,128]{1,0:T(8,128)(2,1)} custom-call(s32[720]{0:T(1024)} %reshape.103.list_ref, s32[6]{0:T(128)} %get-tuple-element.14.count_ref, bf16[768,128]{1,0:T(8,128)(2,1)} %copy.50.q_ref, s32[768,1]{1,0:T(8,128)} %bitcast.69, bf16[96,128,256]{2,1,0:T(8,128)(2,1)} %bitcast.64, s32[96,1,128]{2,1,0:T(1,128)} %bitcast.83), custom_call_target="tpu_custom_call" | custom-call | tf_op jit(solution)/shard_map/pallas_call | solution.py:158
  112.7 1.1 copy.52
  113.8 1.2 broadcast_in_dim.12
  115.0 6.5 %all-to-all-start.1 = ((bf16[8,768,128]{1,2,0:T(8,128)(2,1)}), bf16[8,768,128]{1,2,0:T(8,128)(2,1)}, u32[]{:S(2)}, u32[]{:S(2)}) async-start(bf16[8,768,128]{1,2,0:T(8,128)(2,1)} %broadcast_in_dim.12), calls=%async_computation.1 | async-start | bytes 3145728 | tf_op jit(solution)/shard_map/all_to_all | solution.py:192
  121.5 13.1 %all-gather.7.cloned.1.call-done = bf16[4096,512]{1,0:T(8,128)(2,1)} async-done(((bf16[256,512]{1,0:T(8,128)(2,1)}), bf16[4096,512]{1,0:T(8,128)(2,1)}) %all-gather.7.cloned.1.call-update) | async-done | bytes 4194320 | tf_op jit(solution)/shard_map/all_gather | solution.py:46
  134.6 1.8 slice.55
  136.4 2.2 reshape_reshape.6
  138.6 2.8 %fusion.75 = (bf16[16,64,512]{2,1,0:T(8,128)(2,1)S(1)}, bf16[16,64,512]{2,1,0:T(8,128)(2,1)}) fusion(bf16[16,256,512]{2,1,0:T(8,128)(2,1)} %bitcast.67), kind=kLoop, calls=%fused_computation.111 | loop fusion | bytes 4194304 | tf_op jit(solution)/shard_map/slice | solution.py:49
  141.5 6.2 %all-to-all-done.1 = bf16[8,768,128]{1,2,0:T(8,128)(2,1)} async-done(((bf16[8,768,128]{1,2,0:T(8,128)(2,1)}), bf16[8,768,128]{1,2,0:T(8,128)(2,1)}, u32[]{:S(2)}, u32[]{:S(2)}) %all-to-all-start.1) | async-done | bytes 1572896 | tf_op jit(solution)/shard_map/all_to_all | solution.py:192
  147.6 3.8 %fusion.79 = (f32[768]{0:T(1024)S(1)}, f32[768,1024]{1,0:T(8,128)S(1)}) fusion(bf16[768,1024]{0,1:T(8,128)(2,1)} %bitcast.24, bf16[1024,1024]{1,0:T(8,128)(2,1)S(1)} %copy-done, bf16[768,1024]{1,0:T(8,128)(2,1)} %param.6), kind=kOutput, calls=%fused_computation.115 | convolution fusion | flops 1612971264 | bytes 8391680 | tf_op jit(solution)/shard_map/dot_general | solution.py:194
  152.3 7.3 %convolution_convert_fusion = bf16[768,1024]{1,0:T(8,128)(2,1)} fusion(bf16[1024,512]{1,0:T(8,128)(2,1)} %bitcast.74, bf16[768,1024]{1,0:T(8,128)(2,1)S(1)} %multiply_convert_fusion, bf16[1024,512]{1,0:T(8,128)(2,1)S(1)} %bitcast.73), kind=kOutput, calls=%fused_computation.5 | convolution fusion | flops 1636958208 | bytes 5242880 | tf_op jit(solution)/shard_map/dot_general | solution.py:202
  159.6 3.6 %all-to-all-start.2 = ((bf16[8,96,1024]{2,1,0:T(8,128)(2,1)}), bf16[8,96,1024]{2,1,0:T(8,128)(2,1)S(1)}, u32[]{:S(2)}, u32[]{:S(2)}) async-start(bf16[8,96,1024]{2,1,0:T(8,128)(2,1)} %bitcast.68), calls=%async_computation.2 | async-start | bytes 3145728 | tf_op jit(solution)/shard_map/all_to_all | solution.py:57
  163.2 0.8 compare_convert_fusion
  164.0 21.6 %all-to-all-done.2 = bf16[8,96,1024]{2,1,0:T(8,128)(2,1)S(1)} async-done(((bf16[8,96,1024]{2,1,0:T(8,128)(2,1)}), bf16[8,96,1024]{2,1,0:T(8,128)(2,1)S(1)}, u32[]{:S(2)}, u32[]{:S(2)}) %all-to-all-start.2) | async-done | bytes 1572896 | tf_op jit(solution)/shard_map/all_to_all | solution.py:57
  186.6 25.5 %all_to_all.38 = bf16[8,96,1024]{2,1,0:T(8,128)(2,1)S(1)} all-to-all(bf16[8,96,1024]{2,1,0:T(8,128)(2,1)S(1)} %broadcast_in_dim.13), channel_id=1, replica_groups=mesh['dp'=16,'tensor'=8] {'tensor'}, dimensions={0} | all-to-all | bytes 3145728 | tf_op jit(solution)/shard_map/all_to_all | solution.py:64
  212.1 1.1 copy.66
  (51 shorter events, 4.3 us)
Async XLA Ops:
  6.5 84.4 %all-gather.5.cloned.1.call-start = ((), (), s32[]{:S(2)}) async-start(), calls=%async_computation.4 | async-start | bytes 6684672 | tf_op jit(solution)/shard_map/all_gather | solution.py:183
  28.1 22.7 %copy-start.2 = (bf16[768,1024]{1,0:T(8,128)(2,1)S(1)}, bf16[768,1024]{1,0:T(8,128)(2,1)}, u32[]{:S(2)}) copy-start(bf16[768,1024]{1,0:T(8,128)(2,1)} %param.6) | copy-start | bytes 4718596
  52.0 1.9 copy-start.1
  52.9 81.7 %all-gather.7.cloned.1.call-start = ((), (), s32[]{:S(2)}) async-start(), calls=%async_computation.5 | async-start | bytes 4456448 | tf_op jit(solution)/shard_map/all_gather | solution.py:46
  115.0 32.6 %all-to-all-start.1 = ((bf16[8,768,128]{1,2,0:T(8,128)(2,1)}), bf16[8,768,128]{1,2,0:T(8,128)(2,1)}, u32[]{:S(2)}, u32[]{:S(2)}) async-start(bf16[8,768,128]{1,2,0:T(8,128)(2,1)} %broadcast_in_dim.12), calls=%async_computation.1 | async-start | bytes 3145728 | tf_op jit(solution)/shard_map/all_to_all | solution.py:192
  138.6 9.0 %copy-start = (bf16[1024,1024]{1,0:T(8,128)(2,1)S(1)}, bf16[1024,1024]{1,0:T(8,128)(2,1)}, u32[]{:S(2)}) copy-start(bf16[1024,1024]{1,0:T(8,128)(2,1)} %reshape_reshape.6) | copy-start | bytes 6291460
  159.6 26.0 %all-to-all-start.2 = ((bf16[8,96,1024]{2,1,0:T(8,128)(2,1)}), bf16[8,96,1024]{2,1,0:T(8,128)(2,1)S(1)}, u32[]{:S(2)}, u32[]{:S(2)}) async-start(bf16[8,96,1024]{2,1,0:T(8,128)(2,1)} %bitcast.68), calls=%async_computation.2 | async-start | bytes 3145728 | tf_op jit(solution)/shard_map/all_to_all | solution.py:57
Sparse Core Ops, SparseCore 0:
  53.0 37.8 all-gather.4
  92.6 41.9 all-gather.6

commit v9 on v8

--- a/solution.py
+++ b/solution.py
@@ -80,7 +80,7 @@
     lane_head = lax.broadcasted_iota(jnp.int32, q.shape, 1) // HEAD
     stacked_q = jnp.concatenate(
         [jnp.where(lane_head == h, q, jnp.zeros_like(q)) for h in range(heads)], axis=0
-    )
+    ) * jnp.asarray(scale, q.dtype)
     qid = qid_ref[...]
     stacked_id = jnp.concatenate([qid] * heads, axis=0)
     count = count_ref[i]
@@ -96,11 +96,13 @@
         k = kv[:, :width]
         v = kv[:, width:]
         kid = jnp.concatenate([kid_ref[kp] for kp in kps], axis=1)
-        allowed = jnp.logical_and(stacked_id == kid, slot_chunk + base < count)
+        allowed = stacked_id == kid
+        if pages % CHUNK:
+            allowed = jnp.logical_and(allowed, slot_chunk + base < count)
         s = lax.dot_general(
             stacked_q, k, (((1,), (1,)), ((), ())), preferred_element_type=jnp.float32
         )
-        s = jnp.where(allowed, s * scale, -jnp.inf)
+        s = jnp.where(allowed, s, -jnp.inf)
         m_old = m_ref[...]
         m_new = jnp.maximum(m_old, jnp.max(s, axis=1, keepdims=True))
         p = jnp.exp(s - m_new)

time: 220 us -> 220 us (level)
  Pallas kernels: 21.8 us -> 16.3 us
  waiting for transfers between devices: 72.3 us -> 76.1 us
    all_gather x1, waiting for transfers between devices: 13.1 us -> 20.3 us  [spread_weights(): all_rest = lax.all_gather(rest, 'dp', axis=0, tiled=False)]
    pallas_call x1, Pallas kernels: 21.8 us -> 16.3 us  [paged_attention(): pl.pallas_call(attention_kernel, grid_spec=grid_spec, out_shape=jax.Shape...]
    all_to_all x1, waiting for transfers between devices: 6.18 us -> 1.7 us  [shards(): lax.all_to_all(spread, 'tensor', 0, 2, tiled=True).reshape(tok_rows, -1)]
  transfers between devices with their start and end apart: 4 -> 4, of which waited for: 4 -> 4; matrix products, arithmetic and copies ran while one was open for 7% -> 7% of each run, Pallas kernels for 10% -> 7%
where the time goes in v9:
time: 220 us; the launch traced here: 219 us
  waiting for transfers between devices  76.1 us (35%)
  blocking collectives  65.1 us (30%)
  Pallas kernels  16.3 us (7%)
  local copies, waits for them, and re-layouts  14.9 us (7%)
  between operations  13.6 us (6%)
  matrix products  12.9 us (6%)
  starting transfers between devices  10.3 us (5%)
  other arithmetic  10.2 us (5%)
    all_gather x1, waiting for transfers between devices, shards(): lax.all_gather(kv_rows, 'dp', axis=0, tiled=False)  31.5 us
    all_to_all x1, blocking collectives, gather_rows(): lax.all_to_all(spread, 'tensor', 0, 0, tiled=True)  26.5 us
    all_to_all x1, waiting for transfers between devices, sum_scatter(): lax.all_to_all(part.reshape(groups, -1, part.shape[1]), 'tensor', 0, 0, t...  22.5 us
    all_gather x1, blocking collectives, spread_weights(): qkv_block = lax.all_gather(qkv_local, 'dp', axis=0, tiled=True)  22.3 us
    all_gather x1, waiting for transfers between devices, spread_weights(): all_rest = lax.all_gather(rest, 'dp', axis=0, tiled=False)  20.3 us
    pallas_call x1, Pallas kernels, paged_attention(): pl.pallas_call(attention_kernel, grid_spec=grid_spec, out_shape=jax.Shape...  16.3 us
    all_to_all x1, blocking collectives, spread_weights(): lax.all_to_all(jnp.concatenate(parts, axis=1), 'tensor', 0, 0, tiled=True)  16.3 us
    dot_general x1, matrix products, shards(): lax.dot_general(inner, down_cols, (((1,), (1,)), ((), ())), preferred_ele...  7.32 us
  transfers between devices with their start and end apart: 4, of which 4 were waited for; matrix products, arithmetic and copies ran while one was open for 7% of the time, Pallas kernels for 7%

profile of v9, /device:TPU:0, one launch (start us, length us, event | category | flops | bytes accessed | tf_op | source)
XLA Modules:
  0.0 219.5 jit_solution(15629047450514069859)
XLA Ops:
  6.5 0.9 convert_element_type.50
  7.5 0.9 convert_element_type.49
  8.4 0.9 convert_element_type.48
  9.3 0.8 convert_bitcast_fusion
  10.7 0.8 reduce
  11.8 16.3 %all_to_all.37 = bf16[8,2,9728]{2,1,0:T(2,128)(2,1)S(1)} all-to-all(bf16[8,2,9728]{2,1,0:T(2,128)(2,1)S(1)} %reshape.127), channel_id=1, replica_groups=mesh['dp'=16,'tensor'=8] {'tensor'}, dimensions={0} | all-to-all | bytes 622592 | tf_op jit(solution)/shard_map/all_to_all | solution.py:36
  28.5 22.3 %all_gather.15 = bf16[1024,384]{1,0:T(8,128)(2,1)S(1)} all-gather(bf16[64,384]{1,0:T(8,128)(2,1)S(1)} %reshape.110), channel_id=1, replica_groups=mesh['dp'=16,'tensor'=8] {'dp'}, dimensions={0}, use_global_device_ids=true | all-gather | bytes 835584 | tf_op jit(solution)/shard_map/all_gather | solution.py:44
  50.8 0.9 convolution_convert_fusion.1
  52.0 0.8 pad_maximum_fusion
  53.1 0.7 pad_maximum_fusion.1
  54.1 1.0 fusion.78
  55.2 1.5 sort.17
  57.0 0.7 reshape.103.list_ref
  57.7 0.9 copy.57
  58.6 0.8 copy.50.q_ref
  59.4 31.5 %all-gather.5.cloned.1.call-done = bf16[12288,256]{1,0:T(8,128)(2,1)} async-done(((bf16[768,256]{1,0:T(8,128)(2,1)}), bf16[12288,256]{1,0:T(8,128)(2,1)}) %all-gather.5.cloned.1.call-update) | async-done | bytes 6291472 | tf_op jit(solution)/shard_map/all_gather | solution.py:185
  90.9 16.3 %shard_map.64 = bf16[768,128]{1,0:T(8,128)(2,1)} custom-call(s32[720]{0:T(1024)} %reshape.103.list_ref, s32[6]{0:T(128)} %get-tuple-element.14.count_ref, bf16[768,128]{1,0:T(8,128)(2,1)} %copy.50.q_ref, s32[768,1]{1,0:T(8,128)} %bitcast.69, bf16[96,128,256]{2,1,0:T(8,128)(2,1)} %bitcast.64, s32[96,1,128]{2,1,0:T(1,128)} %bitcast.83), custom_call_target="tpu_custom_call" | custom-call | tf_op jit(solution)/shard_map/pallas_call | solution.py:160
  107.2 1.1 copy.52
  108.3 1.2 broadcast_in_dim.12
  109.5 6.5 %all-to-all-start.1 = ((bf16[8,768,128]{1,2,0:T(8,128)(2,1)}), bf16[8,768,128]{1,2,0:T(8,128)(2,1)}, u32[]{:S(2)}, u32[]{:S(2)}) async-start(bf16[8,768,128]{1,2,0:T(8,128)(2,1)} %broadcast_in_dim.12), calls=%async_computation.1 | async-start | bytes 3145728 | tf_op jit(solution)/shard_map/all_to_all | solution.py:194
  116.0 20.3 %all-gather.7.cloned.1.call-done = bf16[4096,512]{1,0:T(8,128)(2,1)} async-done(((bf16[256,512]{1,0:T(8,128)(2,1)}), bf16[4096,512]{1,0:T(8,128)(2,1)}) %all-gather.7.cloned.1.call-update) | async-done | bytes 4194320 | tf_op jit(solution)/shard_map/all_gather | solution.py:46
  136.4 1.8 slice.55
  138.2 2.2 reshape_reshape.6
  140.4 2.8 %fusion.75 = (bf16[16,64,512]{2,1,0:T(8,128)(2,1)S(1)}, bf16[16,64,512]{2,1,0:T(8,128)(2,1)}) fusion(bf16[16,256,512]{2,1,0:T(8,128)(2,1)} %bitcast.67), kind=kLoop, calls=%fused_computation.111 | loop fusion | bytes 4194304 | tf_op jit(solution)/shard_map/slice | solution.py:49
  143.2 1.7 all-to-all-done.1
  144.9 3.8 %fusion.79 = (f32[768]{0:T(1024)S(1)}, f32[768,1024]{1,0:T(8,128)S(1)}) fusion(bf16[768,1024]{0,1:T(8,128)(2,1)} %bitcast.24, bf16[1024,1024]{1,0:T(8,128)(2,1)S(1)} %copy-done, bf16[768,1024]{1,0:T(8,128)(2,1)} %param.6), kind=kOutput, calls=%fused_computation.115 | convolution fusion | flops 1612971264 | bytes 8391680 | tf_op jit(solution)/shard_map/dot_general | solution.py:196
  149.6 7.3 %convolution_convert_fusion = bf16[768,1024]{1,0:T(8,128)(2,1)} fusion(bf16[1024,512]{1,0:T(8,128)(2,1)} %bitcast.74, bf16[768,1024]{1,0:T(8,128)(2,1)S(1)} %multiply_convert_fusion, bf16[1024,512]{1,0:T(8,128)(2,1)S(1)} %bitcast.73), kind=kOutput, calls=%fused_computation.5 | convolution fusion | flops 1636958208 | bytes 5242880 | tf_op jit(solution)/shard_map/dot_general | solution.py:204
  156.9 3.8 %all-to-all-start.2 = ((bf16[8,96,1024]{2,1,0:T(8,128)(2,1)}), bf16[8,96,1024]{2,1,0:T(8,128)(2,1)S(1)}, u32[]{:S(2)}, u32[]{:S(2)}) async-start(bf16[8,96,1024]{2,1,0:T(8,128)(2,1)} %bitcast.68), calls=%async_computation.2 | async-start | bytes 3145728 | tf_op jit(solution)/shard_map/all_to_all | solution.py:57
  160.7 0.8 compare_convert_fusion
  161.4 22.5 %all-to-all-done.2 = bf16[8,96,1024]{2,1,0:T(8,128)(2,1)S(1)} async-done(((bf16[8,96,1024]{2,1,0:T(8,128)(2,1)}), bf16[8,96,1024]{2,1,0:T(8,128)(2,1)S(1)}, u32[]{:S(2)}, u32[]{:S(2)}) %all-to-all-start.2) | async-done | bytes 1572896 | tf_op jit(solution)/shard_map/all_to_all | solution.py:57
  185.0 26.5 %all_to_all.38 = bf16[8,96,1024]{2,1,0:T(8,128)(2,1)S(1)} all-to-all(bf16[8,96,1024]{2,1,0:T(8,128)(2,1)S(1)} %broadcast_in_dim.13), channel_id=1, replica_groups=mesh['dp'=16,'tensor'=8] {'tensor'}, dimensions={0} | all-to-all | bytes 3145728 | tf_op jit(solution)/shard_map/all_to_all | solution.py:64
  211.5 1.1 copy.66
  (51 shorter events, 4.3 us)
Async XLA Ops:
  6.5 84.4 %all-gather.5.cloned.1.call-start = ((), (), s32[]{:S(2)}) async-start(), calls=%async_computation.4 | async-start | bytes 6684672 | tf_op jit(solution)/shard_map/all_gather | solution.py:185
  28.1 22.7 %copy-start.2 = (bf16[768,1024]{1,0:T(8,128)(2,1)S(1)}, bf16[768,1024]{1,0:T(8,128)(2,1)}, u32[]{:S(2)}) copy-start(bf16[768,1024]{1,0:T(8,128)(2,1)} %param.6) | copy-start | bytes 4718596
  52.0 1.9 copy-start.1
  52.9 83.5 %all-gather.7.cloned.1.call-start = ((), (), s32[]{:S(2)}) async-start(), calls=%async_computation.5 | async-start | bytes 4456448 | tf_op jit(solution)/shard_map/all_gather | solution.py:46
  109.5 35.4 %all-to-all-start.1 = ((bf16[8,768,128]{1,2,0:T(8,128)(2,1)}), bf16[8,768,128]{1,2,0:T(8,128)(2,1)}, u32[]{:S(2)}, u32[]{:S(2)}) async-start(bf16[8,768,128]{1,2,0:T(8,128)(2,1)} %broadcast_in_dim.12), calls=%async_computation.1 | async-start | bytes 3145728 | tf_op jit(solution)/shard_map/all_to_all | solution.py:194
  140.4 4.6 %copy-start = (bf16[1024,1024]{1,0:T(8,128)(2,1)S(1)}, bf16[1024,1024]{1,0:T(8,128)(2,1)}, u32[]{:S(2)}) copy-start(bf16[1024,1024]{1,0:T(8,128)(2,1)} %reshape_reshape.6) | copy-start | bytes 6291460
  156.9 27.1 %all-to-all-start.2 = ((bf16[8,96,1024]{2,1,0:T(8,128)(2,1)}), bf16[8,96,1024]{2,1,0:T(8,128)(2,1)S(1)}, u32[]{:S(2)}, u32[]{:S(2)}) async-start(bf16[8,96,1024]{2,1,0:T(8,128)(2,1)} %bitcast.68), calls=%async_computation.2 | async-start | bytes 3145728 | tf_op jit(solution)/shard_map/all_to_all | solution.py:57
Sparse Core Ops, SparseCore 0:
  53.0 37.8 all-gather.4
  92.6 43.7 all-gather.6

commit v10 on v8

--- a/solution.py
+++ b/solution.py
@@ -42,13 +42,14 @@
     down_local = piece[2].reshape(-1, width)
     out_local = piece[3].reshape(-1, width)
     qkv_block = lax.all_gather(qkv_local, "dp", axis=0, tiled=True)
-    rest = jnp.concatenate([up_local, down_local, out_local], axis=0)
+    all_out = lax.all_gather(out_local, "dp", axis=0, tiled=False)
+    rest = jnp.concatenate([up_local, down_local], axis=0)
     all_rest = lax.all_gather(rest, "dp", axis=0, tiled=False)
     dp_size = all_rest.shape[0]
-    offs = [0, up_local.shape[0], up_local.shape[0] + down_local.shape[0], rest.shape[0]]
-    up_block = all_rest[:, offs[0]:offs[1]].reshape(dp_size * up_local.shape[0], width)
-    down_full = all_rest[:, offs[1]:offs[2]].reshape(dp_size, groups, cols, -1)
-    out_full = all_rest[:, offs[2]:offs[3]].reshape(dp_size, groups, cols, -1)
+    up_rows = up_local.shape[0]
+    up_block = all_rest[:, :up_rows].reshape(dp_size * up_rows, width)
+    down_full = all_rest[:, up_rows:].reshape(dp_size, groups, cols, -1)
+    out_full = all_out.reshape(dp_size, groups, cols, -1)
     return qkv_block, up_block, down_full, out_full
 
 

time: 220 us -> 243 us (1.10)
  waiting for transfers between devices: 72.3 us -> 95.4 us
  starting transfers between devices: 10.1 us -> 13.5 us
  Pallas kernels: 21.8 us -> 18.5 us
    all_gather x1, waiting for transfers between devices: 13.1 us -> 31.9 us  [spread_weights(): all_rest = lax.all_gather(rest, 'dp', axis=0, tiled=False)]
    all_gather x0 -> x1, waiting for transfers between devices: none -> 10.2 us  [spread_weights(): all_out = lax.all_gather(out_local, 'dp', axis=0, tiled=False)]
    all_to_all x1, waiting for transfers between devices: 6.18 us -> 0.01 us  [shards(): lax.all_to_all(spread, 'tensor', 0, 2, tiled=True).reshape(tok_rows, -1)]
    all_to_all x1, starting transfers between devices: 3.58 us -> 6.96 us  [sum_scatter(): lax.all_to_all(part.reshape(groups, -1, part.shape[1]), 'tensor', 0, 0, t...]
    pallas_call x1, Pallas kernels: 21.8 us -> 18.5 us  [paged_attention(): pl.pallas_call(attention_kernel, grid_spec=grid_spec, out_shape=jax.Shape...]
  transfers between devices with their start and end apart: 4 -> 5, of which waited for: 4 -> 4; matrix products, arithmetic and copies ran while one was open for 7% -> 6% of each run, Pallas kernels for 10% -> 8%
where the time goes in v10:
time: 243 us; the launch traced here: 242 us
  waiting for transfers between devices  95.4 us (39%)
  blocking collectives  64.1 us (26%)
  Pallas kernels  18.5 us (8%)
  local copies, waits for them, and re-layouts  14.1 us (6%)
  starting transfers between devices  13.5 us (6%)
  between operations  13.3 us (5%)
  matrix products  12.9 us (5%)
  other arithmetic  10.2 us (4%)
    all_gather x1, waiting for transfers between devices, spread_weights(): all_rest = lax.all_gather(rest, 'dp', axis=0, tiled=False)  31.9 us
    all_gather x1, waiting for transfers between devices, shards(): lax.all_gather(kv_rows, 'dp', axis=0, tiled=False)  30.8 us
    all_to_all x1, blocking collectives, gather_rows(): lax.all_to_all(spread, 'tensor', 0, 0, tiled=True)  25.5 us
    all_to_all x1, waiting for transfers between devices, sum_scatter(): lax.all_to_all(part.reshape(groups, -1, part.shape[1]), 'tensor', 0, 0, t...  22.5 us
    all_gather x1, blocking collectives, spread_weights(): qkv_block = lax.all_gather(qkv_local, 'dp', axis=0, tiled=True)  22.3 us
    pallas_call x1, Pallas kernels, paged_attention(): pl.pallas_call(attention_kernel, grid_spec=grid_spec, out_shape=jax.Shape...  18.5 us
    all_to_all x1, blocking collectives, spread_weights(): lax.all_to_all(jnp.concatenate(parts, axis=1), 'tensor', 0, 0, tiled=True)  16.3 us
    all_gather x1, waiting for transfers between devices, spread_weights(): all_out = lax.all_gather(out_local, 'dp', axis=0, tiled=False)  10.2 us
  transfers between devices with their start and end apart: 5, of which 4 were waited for; matrix products, arithmetic and copies ran while one was open for 6% of the time, Pallas kernels for 8%

profile of v10, /device:TPU:0, one launch (start us, length us, event | category | flops | bytes accessed | tf_op | source)
XLA Modules:
  0.0 242.1 jit_solution(2629506311760776927)
XLA Ops:
  6.5 0.9 convert_element_type.50
  7.5 0.9 convert_element_type.49
  8.4 0.9 convert_element_type.48
  9.3 0.8 convert_bitcast_fusion
  10.7 0.8 reduce
  11.8 16.3 %all_to_all.37 = bf16[8,2,9728]{2,1,0:T(2,128)(2,1)S(1)} all-to-all(bf16[8,2,9728]{2,1,0:T(2,128)(2,1)S(1)} %reshape.123), channel_id=1, replica_groups=mesh['dp'=16,'tensor'=8] {'tensor'}, dimensions={0} | all-to-all | bytes 622592 | tf_op jit(solution)/shard_map/all_to_all | solution.py:36
  28.5 22.3 %all_gather.18 = bf16[1024,384]{1,0:T(8,128)(2,1)S(1)} all-gather(bf16[64,384]{1,0:T(8,128)(2,1)S(1)} %reshape.107), channel_id=1, replica_groups=mesh['dp'=16,'tensor'=8] {'dp'}, dimensions={0}, use_global_device_ids=true | all-gather | bytes 835584 | tf_op jit(solution)/shard_map/all_gather | solution.py:44
  50.8 0.9 convolution_convert_fusion.1
  52.0 0.8 pad_maximum_fusion
  52.9 0.7 all_gather_reshape.3
  53.8 0.7 pad_maximum_fusion.1
  54.8 1.0 fusion.78
  55.9 1.5 sort.17
  57.6 0.7 reshape.100.list_ref
  58.3 0.9 copy.57
  59.3 0.8 copy.50.q_ref
  60.1 30.8 %all-gather.8.cloned.1.call-done = bf16[12288,256]{1,0:T(8,128)(2,1)} async-done(((bf16[768,256]{1,0:T(8,128)(2,1)}), bf16[12288,256]{1,0:T(8,128)(2,1)}) %all-gather.8.cloned.1.call-update) | async-done | bytes 6291472 | tf_op jit(solution)/shard_map/all_gather | solution.py:184
  90.9 18.5 %shard_map.64 = bf16[768,128]{1,0:T(8,128)(2,1)} custom-call(s32[720]{0:T(1024)} %reshape.100.list_ref, s32[6]{0:T(128)} %get-tuple-element.14.count_ref, bf16[768,128]{1,0:T(8,128)(2,1)} %copy.50.q_ref, s32[768,1]{1,0:T(8,128)} %bitcast.68, bf16[96,128,256]{2,1,0:T(8,128)(2,1)} %bitcast.64, s32[96,1,128]{2,1,0:T(1,128)} %bitcast.82), custom_call_target="tpu_custom_call" | custom-call | tf_op jit(solution)/shard_map/pallas_call | solution.py:159
  109.4 1.1 copy.52
  110.5 1.2 broadcast_in_dim.12
  111.7 6.5 %all-to-all-start.1 = ((bf16[8,768,128]{1,2,0:T(8,128)(2,1)}), bf16[8,768,128]{1,2,0:T(8,128)(2,1)}, u32[]{:S(2)}, u32[]{:S(2)}) async-start(bf16[8,768,128]{1,2,0:T(8,128)(2,1)} %broadcast_in_dim.12), calls=%async_computation.1 | async-start | bytes 3145728 | tf_op jit(solution)/shard_map/all_to_all | solution.py:193
  118.2 10.2 %all-gather.6.cloned.1.call-done = bf16[16,128,512]{2,1,0:T(8,128)(2,1)} async-done(((bf16[1,128,512]{2,1,0:T(8,128)(2,1)}), bf16[16,128,512]{2,1,0:T(8,128)(2,1)}) %all-gather.6.cloned.1.call-update) | async-done | bytes 2097168 | tf_op jit(solution)/shard_map/all_gather | solution.py:45
  128.4 2.7 %reshape_reshape.6 = bf16[1024,1024]{1,0:T(8,128)(2,1)S(1)} reshape(bf16[16,128,512]{2,1,0:T(8,128)(2,1)} %all-gather.6.cloned.1.call-done) | data formatting | bytes 4194304 | tf_op jit(solution)/shard_map/reshape;reshape | solution.py:194
  131.1 31.9 %all-gather.10.cloned.1.call-done = bf16[2048,512]{1,0:T(8,128)(2,1)} async-done(((bf16[128,512]{1,0:T(8,128)(2,1)}), bf16[2048,512]{1,0:T(8,128)(2,1)}) %all-gather.10.cloned.1.call-update) | async-done | bytes 2097168 | tf_op jit(solution)/shard_map/all_gather | solution.py:47
  163.0 2.7 %fusion.75 = (bf16[16,64,512]{2,1,0:T(8,128)(2,1)S(1)}, bf16[16,64,512]{2,1,0:T(8,128)(2,1)}) fusion(bf16[16,128,512]{2,1,0:T(8,128)(2,1)} %bitcast.66), kind=kLoop, calls=%fused_computation.111 | loop fusion | bytes 4194304 | tf_op jit(solution)/shard_map/slice | solution.py:50
  165.7 3.8 %fusion.79 = (f32[768]{0:T(1024)S(1)}, f32[768,1024]{1,0:T(8,128)S(1)}) fusion(bf16[768,1024]{0,1:T(8,128)(2,1)} %bitcast.24, bf16[1024,1024]{1,0:T(8,128)(2,1)S(1)} %reshape_reshape.6, bf16[768,1024]{1,0:T(8,128)(2,1)} %param.6), kind=kOutput, calls=%fused_computation.115 | convolution fusion | flops 1612971264 | bytes 8391680 | tf_op jit(solution)/shard_map/dot_general | solution.py:195
  170.3 7.3 %convolution_convert_fusion = bf16[768,1024]{1,0:T(8,128)(2,1)} fusion(bf16[1024,512]{1,0:T(8,128)(2,1)} %bitcast.73, bf16[768,1024]{1,0:T(8,128)(2,1)S(1)} %multiply_convert_fusion, bf16[1024,512]{1,0:T(8,128)(2,1)S(1)} %bitcast.72), kind=kOutput, calls=%fused_computation.5 | convolution fusion | flops 1636958208 | bytes 5242880 | tf_op jit(solution)/shard_map/dot_general | solution.py:203
  177.7 7.0 %all-to-all-start.2 = ((bf16[8,96,1024]{2,1,0:T(8,128)(2,1)}), bf16[8,96,1024]{2,1,0:T(8,128)(2,1)S(1)}, u32[]{:S(2)}, u32[]{:S(2)}) async-start(bf16[8,96,1024]{2,1,0:T(8,128)(2,1)} %bitcast.67), calls=%async_computation.2 | async-start | bytes 3145728 | tf_op jit(solution)/shard_map/all_to_all | solution.py:58
  184.6 0.8 compare_convert_fusion
  185.4 22.5 %all-to-all-done.2 = bf16[8,96,1024]{2,1,0:T(8,128)(2,1)S(1)} async-done(((bf16[8,96,1024]{2,1,0:T(8,128)(2,1)}), bf16[8,96,1024]{2,1,0:T(8,128)(2,1)S(1)}, u32[]{:S(2)}, u32[]{:S(2)}) %all-to-all-start.2) | async-done | bytes 1572896 | tf_op jit(solution)/shard_map/all_to_all | solution.py:58
  208.9 25.5 %all_to_all.38 = bf16[8,96,1024]{2,1,0:T(8,128)(2,1)S(1)} all-to-all(bf16[8,96,1024]{2,1,0:T(8,128)(2,1)S(1)} %broadcast_in_dim.13), channel_id=1, replica_groups=mesh['dp'=16,'tensor'=8] {'tensor'}, dimensions={0} | all-to-all | bytes 3145728 | tf_op jit(solution)/shard_map/all_to_all | solution.py:65
  234.4 1.1 copy.66
  (51 shorter events, 4.3 us)
Async XLA Ops:
  6.5 84.3 %all-gather.8.cloned.1.call-start = ((), (), s32[]{:S(2)}) async-start(), calls=%async_computation.5 | async-start | bytes 6684672 | tf_op jit(solution)/shard_map/all_gather | solution.py:184
  28.1 22.7 %copy-start.1 = (bf16[768,1024]{1,0:T(8,128)(2,1)S(1)}, bf16[768,1024]{1,0:T(8,128)(2,1)}, u32[]{:S(2)}) copy-start(bf16[768,1024]{1,0:T(8,128)(2,1)} %param.6) | copy-start | bytes 4718596
  51.8 2.7 %copy-start = (s32[96,128]{1,0:T(8,128)S(1)}, s32[96,128]{1,0:T(8,128)}, u32[]{:S(2)}) copy-start(s32[96,128]{1,0:T(8,128)} %param.11) | copy-start | bytes 147460
  52.9 75.5 %all-gather.6.cloned.1.call-start = ((), (), s32[]{:S(2)}) async-start(), calls=%async_computation.4 | async-start | bytes 2228224 | tf_op jit(solution)/shard_map/all_gather | solution.py:45
  53.7 109.3 %all-gather.10.cloned.1.call-start = ((), (), s32[]{:S(2)}) async-start(), calls=%async_computation.6 | async-start | bytes 2228224 | tf_op jit(solution)/shard_map/all_gather | solution.py:47
  111.7 54.0 %all-to-all-start.1 = ((bf16[8,768,128]{1,2,0:T(8,128)(2,1)}), bf16[8,768,128]{1,2,0:T(8,128)(2,1)}, u32[]{:S(2)}, u32[]{:S(2)}) async-start(bf16[8,768,128]{1,2,0:T(8,128)(2,1)} %broadcast_in_dim.12), calls=%async_computation.1 | async-start | bytes 3145728 | tf_op jit(solution)/shard_map/all_to_all | solution.py:193
  177.7 30.2 %all-to-all-start.2 = ((bf16[8,96,1024]{2,1,0:T(8,128)(2,1)}), bf16[8,96,1024]{2,1,0:T(8,128)(2,1)S(1)}, u32[]{:S(2)}, u32[]{:S(2)}) async-start(bf16[8,96,1024]{2,1,0:T(8,128)(2,1)} %bitcast.67), calls=%async_computation.2 | async-start | bytes 3145728 | tf_op jit(solution)/shard_map/all_to_all | solution.py:58
Sparse Core Ops, SparseCore 0:
  53.0 37.8 all-gather.7
  92.6 35.7 all-gather.5
  130.1 32.8 all-gather.9

commit v11 on v8

--- a/solution.py
+++ b/solution.py
@@ -66,7 +66,7 @@
 
 HEAD = D // H
 INTERPRET = False
-CHUNK = 24
+CHUNK = 20
 
 
 def attention_kernel(list_ref, count_ref, q_ref, qid_ref, kv_ref, kid_ref, o_ref, m_ref, l_ref, acc_ref):

time: 220 us -> 222 us (level)
  the two profiles are of different devices: /device:TPU:0 before, /device:TPU:2 now
where the time goes in v11:
time: 222 us; the launch traced here: 221 us
  waiting for transfers between devices  72.6 us (33%)
  blocking collectives  64.2 us (29%)
  Pallas kernels  22.6 us (10%)
  local copies, waits for them, and re-layouts  14.9 us (7%)
  between operations  13.6 us (6%)
  matrix products  12.9 us (6%)
  other arithmetic  10.2 us (5%)
  starting transfers between devices  9.43 us (4%)
    all_gather x1, waiting for transfers between devices, shards(): lax.all_gather(kv_rows, 'dp', axis=0, tiled=False)  31.3 us
    all_to_all x1, blocking collectives, gather_rows(): lax.all_to_all(spread, 'tensor', 0, 0, tiled=True)  25.8 us
    all_to_all x1, waiting for transfers between devices, sum_scatter(): lax.all_to_all(part.reshape(groups, -1, part.shape[1]), 'tensor', 0, 0, t...  23.3 us
    all_gather x1, blocking collectives, spread_weights(): qkv_block = lax.all_gather(qkv_local, 'dp', axis=0, tiled=True)  23.1 us
    pallas_call x1, Pallas kernels, paged_attention(): pl.pallas_call(attention_kernel, grid_spec=grid_spec, out_shape=jax.Shape...  22.6 us
    all_to_all x1, blocking collectives, spread_weights(): lax.all_to_all(jnp.concatenate(parts, axis=1), 'tensor', 0, 0, tiled=True)  15.3 us
    all_gather x1, waiting for transfers between devices, spread_weights(): all_rest = lax.all_gather(rest, 'dp', axis=0, tiled=False)  10.7 us
    all_to_all x1, waiting for transfers between devices, shards(): lax.all_to_all(spread, 'tensor', 0, 2, tiled=True).reshape(tok_rows, -1)  7.37 us
  transfers between devices with their start and end apart: 4, of which 4 were waited for; matrix products, arithmetic and copies ran while one was open for 7% of the time, Pallas kernels for 10%

profile of v11, /device:TPU:2, one launch (start us, length us, event | category | flops | bytes accessed | tf_op | source)
XLA Modules:
  0.0 220.5 jit_solution(2392853797647193510)
XLA Ops:
  6.5 0.9 convert_element_type.50
  7.5 0.9 convert_element_type.49
  8.4 0.9 convert_element_type.48
  9.3 0.8 convert_bitcast_fusion
  10.7 0.8 reduce
  11.8 15.3 %all_to_all.37 = bf16[8,2,9728]{2,1,0:T(2,128)(2,1)S(1)} all-to-all(bf16[8,2,9728]{2,1,0:T(2,128)(2,1)S(1)} %reshape.127), channel_id=1, replica_groups=mesh['dp'=16,'tensor'=8] {'tensor'}, dimensions={0} | all-to-all | bytes 622592 | tf_op jit(solution)/shard_map/all_to_all | solution.py:36
  27.5 23.1 %all_gather.15 = bf16[1024,384]{1,0:T(8,128)(2,1)S(1)} all-gather(bf16[64,384]{1,0:T(8,128)(2,1)S(1)} %reshape.110), channel_id=1, replica_groups=mesh['dp'=16,'tensor'=8] {'dp'}, dimensions={0}, use_global_device_ids=true | all-gather | bytes 835584 | tf_op jit(solution)/shard_map/all_gather | solution.py:44
  50.6 0.9 convolution_convert_fusion.1
  51.9 0.8 pad_maximum_fusion
  53.0 0.7 pad_maximum_fusion.1
  54.0 1.0 fusion.78
  55.1 1.5 sort.17
  56.8 0.7 reshape.103.list_ref
  57.5 0.9 copy.57
  58.4 0.8 copy.50.q_ref
  59.2 31.3 %all-gather.5.cloned.1.call-done = bf16[12288,256]{1,0:T(8,128)(2,1)} async-done(((bf16[768,256]{1,0:T(8,128)(2,1)}), bf16[12288,256]{1,0:T(8,128)(2,1)}) %all-gather.5.cloned.1.call-update) | async-done | bytes 6291472 | tf_op jit(solution)/shard_map/all_gather | solution.py:183
  90.5 22.6 %shard_map.64 = bf16[768,128]{1,0:T(8,128)(2,1)} custom-call(s32[696]{0:T(1024)} %reshape.103.list_ref, s32[6]{0:T(128)} %get-tuple-element.14.count_ref, bf16[768,128]{1,0:T(8,128)(2,1)} %copy.50.q_ref, s32[768,1]{1,0:T(8,128)} %bitcast.69, bf16[96,128,256]{2,1,0:T(8,128)(2,1)} %bitcast.64, s32[96,1,128]{2,1,0:T(1,128)} %bitcast.83), custom_call_target="tpu_custom_call" | custom-call | tf_op jit(solution)/shard_map/pallas_call | solution.py:158
  113.1 1.1 copy.52
  114.1 1.2 broadcast_in_dim.12
  115.4 5.8 %all-to-all-start.1 = ((bf16[8,768,128]{1,2,0:T(8,128)(2,1)}), bf16[8,768,128]{1,2,0:T(8,128)(2,1)}, u32[]{:S(2)}, u32[]{:S(2)}) async-start(bf16[8,768,128]{1,2,0:T(8,128)(2,1)} %broadcast_in_dim.12), calls=%async_computation.1 | async-start | bytes 3145728 | tf_op jit(solution)/shard_map/all_to_all | solution.py:192
  121.2 10.7 %all-gather.7.cloned.1.call-done = bf16[4096,512]{1,0:T(8,128)(2,1)} async-done(((bf16[256,512]{1,0:T(8,128)(2,1)}), bf16[4096,512]{1,0:T(8,128)(2,1)}) %all-gather.7.cloned.1.call-update) | async-done | bytes 4194320 | tf_op jit(solution)/shard_map/all_gather | solution.py:46
  131.8 1.8 slice.55
  133.6 2.2 reshape_reshape.6
  135.8 2.8 %fusion.75 = (bf16[16,64,512]{2,1,0:T(8,128)(2,1)S(1)}, bf16[16,64,512]{2,1,0:T(8,128)(2,1)}) fusion(bf16[16,256,512]{2,1,0:T(8,128)(2,1)} %bitcast.67), kind=kLoop, calls=%fused_computation.111 | loop fusion | bytes 4194304 | tf_op jit(solution)/shard_map/slice | solution.py:49
  138.7 7.4 %all-to-all-done.1 = bf16[8,768,128]{1,2,0:T(8,128)(2,1)} async-done(((bf16[8,768,128]{1,2,0:T(8,128)(2,1)}), bf16[8,768,128]{1,2,0:T(8,128)(2,1)}, u32[]{:S(2)}, u32[]{:S(2)}) %all-to-all-start.1) | async-done | bytes 1572896 | tf_op jit(solution)/shard_map/all_to_all | solution.py:192
  146.0 3.8 %fusion.79 = (f32[768]{0:T(1024)S(1)}, f32[768,1024]{1,0:T(8,128)S(1)}) fusion(bf16[768,1024]{0,1:T(8,128)(2,1)} %bitcast.24, bf16[1024,1024]{1,0:T(8,128)(2,1)S(1)} %copy-done, bf16[768,1024]{1,0:T(8,128)(2,1)} %param.6), kind=kOutput, calls=%fused_computation.115 | convolution fusion | flops 1612971264 | bytes 8391680 | tf_op jit(solution)/shard_map/dot_general | solution.py:194
  150.7 7.3 %convolution_convert_fusion = bf16[768,1024]{1,0:T(8,128)(2,1)} fusion(bf16[1024,512]{1,0:T(8,128)(2,1)} %bitcast.74, bf16[768,1024]{1,0:T(8,128)(2,1)S(1)} %multiply_convert_fusion, bf16[1024,512]{1,0:T(8,128)(2,1)S(1)} %bitcast.73), kind=kOutput, calls=%fused_computation.5 | convolution fusion | flops 1636958208 | bytes 5242880 | tf_op jit(solution)/shard_map/dot_general | solution.py:202
  158.0 3.6 %all-to-all-start.2 = ((bf16[8,96,1024]{2,1,0:T(8,128)(2,1)}), bf16[8,96,1024]{2,1,0:T(8,128)(2,1)S(1)}, u32[]{:S(2)}, u32[]{:S(2)}) async-start(bf16[8,96,1024]{2,1,0:T(8,128)(2,1)} %bitcast.68), calls=%async_computation.2 | async-start | bytes 3145728 | tf_op jit(solution)/shard_map/all_to_all | solution.py:57
  161.6 0.8 compare_convert_fusion
  162.4 23.3 %all-to-all-done.2 = bf16[8,96,1024]{2,1,0:T(8,128)(2,1)S(1)} async-done(((bf16[8,96,1024]{2,1,0:T(8,128)(2,1)}), bf16[8,96,1024]{2,1,0:T(8,128)(2,1)S(1)}, u32[]{:S(2)}, u32[]{:S(2)}) %all-to-all-start.2) | async-done | bytes 1572896 | tf_op jit(solution)/shard_map/all_to_all | solution.py:57
  186.8 25.8 %all_to_all.38 = bf16[8,96,1024]{2,1,0:T(8,128)(2,1)S(1)} all-to-all(bf16[8,96,1024]{2,1,0:T(8,128)(2,1)S(1)} %broadcast_in_dim.13), channel_id=1, replica_groups=mesh['dp'=16,'tensor'=8] {'tensor'}, dimensions={0} | all-to-all | bytes 3145728 | tf_op jit(solution)/shard_map/all_to_all | solution.py:64
  212.5 1.1 copy.66
  (51 shorter events, 4.3 us)
Async XLA Ops:
  6.5 84.0 %all-gather.5.cloned.1.call-start = ((), (), s32[]{:S(2)}) async-start(), calls=%async_computation.4 | async-start | bytes 6684672 | tf_op jit(solution)/shard_map/all_gather | solution.py:183
  27.1 23.5 %copy-start.2 = (bf16[768,1024]{1,0:T(8,128)(2,1)S(1)}, bf16[768,1024]{1,0:T(8,128)(2,1)}, u32[]{:S(2)}) copy-start(bf16[768,1024]{1,0:T(8,128)(2,1)} %param.6) | copy-start | bytes 4718596
  51.9 1.9 copy-start.1
  52.7 79.1 %all-gather.7.cloned.1.call-start = ((), (), s32[]{:S(2)}) async-start(), calls=%async_computation.5 | async-start | bytes 4456448 | tf_op jit(solution)/shard_map/all_gather | solution.py:46
  115.4 30.7 %all-to-all-start.1 = ((bf16[8,768,128]{1,2,0:T(8,128)(2,1)}), bf16[8,768,128]{1,2,0:T(8,128)(2,1)}, u32[]{:S(2)}, u32[]{:S(2)}) async-start(bf16[8,768,128]{1,2,0:T(8,128)(2,1)} %broadcast_in_dim.12), calls=%async_computation.1 | async-start | bytes 3145728 | tf_op jit(solution)/shard_map/all_to_all | solution.py:192
  135.8 10.2 %copy-start = (bf16[1024,1024]{1,0:T(8,128)(2,1)S(1)}, bf16[1024,1024]{1,0:T(8,128)(2,1)}, u32[]{:S(2)}) copy-start(bf16[1024,1024]{1,0:T(8,128)(2,1)} %reshape_reshape.6) | copy-start | bytes 6291460
  158.0 27.7 %all-to-all-start.2 = ((bf16[8,96,1024]{2,1,0:T(8,128)(2,1)}), bf16[8,96,1024]{2,1,0:T(8,128)(2,1)S(1)}, u32[]{:S(2)}, u32[]{:S(2)}) async-start(bf16[8,96,1024]{2,1,0:T(8,128)(2,1)} %bitcast.68), calls=%async_computation.2 | async-start | bytes 3145728 | tf_op jit(solution)/shard_map/all_to_all | solution.py:57
Sparse Core Ops, SparseCore 0:
  52.8 37.6 all-gather.4
  92.2 39.5 all-gather.6
